TPU v7x, 256 devices: a whole 4x4x8 slice. The times are simulated.
256 devices in a mesh: seq: 32 (over x, z), tensor: 8 (over y, core).
Axes of the slice: x: 4, y: 4, z: 8, core: 2. Of those that a mesh axis runs over, the one named last changes fastest.
Arguments:
- queries: bfloat16 [10240, 4096], P('seq', 'tensor'), may hold values from -8 to 8
- key_rows: bfloat16 [10240, 1024], P('seq', 'tensor'), may hold values from -8 to 8
- value_rows: bfloat16 [10240, 1024], P('seq', 'tensor'), may hold values from -6 to 6
- out_weight: bfloat16 [4096, 8192], P('tensor', 'seq'), may hold values from -0.09375 to 0.09375
- residual_in: bfloat16 [10240, 8192], P('seq'), may hold values from -0.1796875 to 0.1796875
- norm_gain: bfloat16 [8192], replicated, may hold values from 0.099609375 to 1.8984375
- prompt_lengths: int32 [18], replicated, may hold values from 1 to 5120, 10240 in all
Outputs:
- normed: bfloat16 [10240, 8192], P('seq')
- cache_keys: bfloat16 [22528, 1024], P('seq', 'tensor')
- cache_values: bfloat16 [22528, 1024], P('seq', 'tensor')
Inputs may be any that keep to these rules, and one draw needn't show every extreme that they name: `prompt_lengths`: the 18 lengths sum to 10240, and the largest is 5120.
All inputs are finite; a program needn't handle non-finite values.
Results may differ from a plain program's by a relative error of at most 0.019.
Values may be sent and summed in bfloat16 or wider, within the bound.
No kernel may reach another device: no remote copies, remote signals or barrier semaphores. Data moves between devices by JAX's collectives and lax.ppermute only.
A program may use at most 192 MiB of HBM per device.

v0:
```python
import math

import jax
import jax.numpy as jnp
from jax import lax
from jax.sharding import PartitionSpec as P

HD = 128
PAGE = 128
SLOT_DEV = 704
MAX_PROMPT = 5120


def position_of(stored, per_device, devices):
    half_block = per_device // 2
    device = stored // per_device
    offset = stored % per_device
    return jnp.where(
        offset < half_block,
        device * half_block + offset,
        (2 * devices - 1 - device) * half_block + offset - half_block,
    )


def stored_row(position, per_device, devices):
    half_block = per_device // 2
    block_index = position // half_block
    device = jnp.where(block_index < devices, block_index, 2 * devices - 1 - block_index)
    offset = position % half_block + jnp.where(block_index < devices, 0, half_block)
    return device * per_device + offset


def segment_of(position, lengths):
    doc_ends = jnp.cumsum(lengths, dtype=jnp.int32)
    return jnp.sum(
        (position[:, None] >= doc_ends[None, :]).astype(jnp.int32), axis=1, dtype=jnp.int32
    )


def slot_source(slot_ids, lengths, page_size):
    padded = (lengths + page_size - 1) // page_size * page_size
    page_ends = jnp.cumsum(padded, dtype=jnp.int32)
    page_starts = page_ends - padded
    doc_ends = jnp.cumsum(lengths, dtype=jnp.int32)
    doc_starts = doc_ends - lengths
    before = (slot_ids[:, None] >= page_ends[None, :]).astype(jnp.int32)
    inside = (slot_ids[:, None] >= page_starts[None, :]).astype(jnp.int32) - before
    page_start = jnp.sum(before * padded[None, :], axis=1, dtype=jnp.int32)
    doc_start = jnp.sum(before * lengths[None, :], axis=1, dtype=jnp.int32)
    length = jnp.sum(inside * lengths[None, :], axis=1, dtype=jnp.int32)
    within = slot_ids - page_start
    is_live = within < length
    return (doc_start + within, is_live)


def attend_block(query_block, block_index, kv_pos, lengths, half, kv_local, group_size, window):
    blocks = kv_pos.shape[0]
    start = jnp.clip(block_index - (window - 1), 0, blocks - window)
    kv_win = lax.dynamic_slice_in_dim(kv_pos, start, window, axis=0)
    kv_win = kv_win.reshape(window * half, -1)
    kv_width = kv_win.shape[1] // 2
    key_win = kv_win[:, :kv_width].reshape(window * half, kv_local, HD)
    value_win = kv_win[:, kv_width:].reshape(window * half, kv_local, HD)
    key_position = start * half + jnp.arange(window * half, dtype=jnp.int32)
    query_position = block_index * half + jnp.arange(half, dtype=jnp.int32)
    key_segment = segment_of(key_position, lengths)
    query_segment = segment_of(query_position, lengths)
    allowed = (key_position[None, :] <= query_position[:, None]) & (
        key_segment[None, :] == query_segment[:, None]
    )
    scores = (
        jnp.einsum("qgjd,kgd->gjqk", query_block, key_win, preferred_element_type=jnp.float32)
        * (1.0 / math.sqrt(HD))
    )
    scores = jnp.where(allowed, scores, -1e30)
    top = jnp.max(scores, axis=-1)
    weights = jnp.where(allowed, jnp.exp(scores - top[..., None]), 0.0)
    total = jnp.sum(weights, axis=-1)
    accum = jnp.einsum(
        "gjqk,kgd->gjqd",
        weights.astype(jnp.bfloat16),
        value_win,
        preferred_element_type=jnp.float32,
    )
    return jnp.transpose(accum / total[..., None], (2, 0, 1, 3))


def body(queries, key_rows, value_rows, out_weight, residual_in, norm_gain, prompt_lengths):
    seq_count = lax.axis_size("seq")
    seq_index = lax.axis_index("seq")
    per_device = queries.shape[0]
    half = per_device // 2
    kv_local = key_rows.shape[1] // HD
    group_size = queries.shape[1] // (kv_local * HD)
    kv_width = key_rows.shape[1]
    kv_rows = jnp.concatenate([key_rows, value_rows], axis=1)
    stacked = lax.all_gather(
        jnp.concatenate([kv_rows, out_weight], axis=0), "seq", axis=0, tiled=False
    )
    kv_piece = stacked[:, :per_device].reshape(seq_count * per_device, 2 * kv_width)
    weight_blocks = stacked[:, per_device:]
    halves = kv_piece.reshape(seq_count, 2, half, 2 * kv_width)
    kv_pos = jnp.concatenate([halves[:, 0], halves[::-1, 1]], axis=0)
    window = min(2 * seq_count, (MAX_PROMPT - 1 + half - 1) // half + 1)
    grouped = queries.reshape(2, half, kv_local, group_size, HD)
    first = attend_block(
        grouped[0], seq_index, kv_pos, prompt_lengths, half, kv_local, group_size, window
    )
    second = attend_block(
        grouped[1], 2 * seq_count - 1 - seq_index, kv_pos, prompt_lengths, half, kv_local,
        group_size, window,
    )
    attended = jnp.concatenate([first, second], axis=0)
    attended = attended.reshape(per_device, -1).astype(jnp.bfloat16)
    partial_value = jnp.einsum(
        "qc,jcn->qjn", attended, weight_blocks, preferred_element_type=jnp.float32
    ).reshape(per_device, -1)
    projected = lax.psum(partial_value.astype(jnp.bfloat16), "tensor").astype(jnp.float32)
    hidden = residual_in.astype(jnp.float32) + projected
    mean_square = jnp.mean(hidden * hidden, axis=-1, keepdims=True)
    normed = (hidden * lax.rsqrt(mean_square + 1e-05) * norm_gain.astype(jnp.float32)).astype(
        jnp.bfloat16
    )
    slot_ids = seq_index * SLOT_DEV + jnp.arange(SLOT_DEV, dtype=jnp.int32)
    source, is_live = slot_source(slot_ids, prompt_lengths, PAGE)
    target = stored_row(source, per_device, seq_count)
    empty_cache = jnp.zeros((SLOT_DEV, kv_width), jnp.bfloat16)
    key_piece = kv_piece[:, :kv_width]
    value_piece = kv_piece[:, kv_width:]
    piece_rows = key_piece.shape[0]
    found = is_live & (target >= 0) & (target < piece_rows)
    safe_index = jnp.clip(target, 0, piece_rows - 1)
    cache_keys = jnp.where(found[:, None], jnp.take(key_piece, safe_index, axis=0), empty_cache)
    cache_values = jnp.where(found[:, None], jnp.take(value_piece, safe_index, axis=0), empty_cache)
    return (normed, cache_keys, cache_values)


def solution(mesh):
    return jax.shard_map(
        body,
        mesh=mesh,
        in_specs=(
            P("seq", "tensor"),
            P("seq", "tensor"),
            P("seq", "tensor"),
            P("tensor", "seq"),
            P("seq", None),
            P(),
            P(),
        ),
        out_specs=(P("seq", None), P("seq", "tensor"), P("seq", "tensor")),
        check_vma=False,
    )
```

profile of v0, /device:TPU:1, one launch (start us, length us, event | category | flops | bytes accessed | tf_op | source)
XLA Modules:
  0.0 322.4 jit_solution(16557774456467817671)
XLA Ops:
  7.2 0.0 all-gather.3.cloned.1.call-start
  7.2 1.8 pad_maximum_fusion
  9.0 0.0 all-gather.3.cloned.1.call-update
  9.0 0.0 all-reduce.2.cloned.1.call-start
  9.1 0.7 fusion.65
  9.8 0.1 copy.27
  9.9 0.1 reduce.5
  10.0 0.7 copy.20
  10.8 0.1 reduce.4
  10.9 0.7 convert_element_type.53
  11.7 0.7 fusion.52
  12.3 0.7 fusion.64
  13.0 0.8 fusion.46
  13.9 0.1 convert_reduce_fusion.3
  14.0 0.3 convert_reduce_fusion.1
  14.2 1.0 slice_bitcast_fusion.23
  15.3 1.5 compare_and_fusion
  16.8 122.4 %all-gather.3.cloned.1.call-done = bf16[26624,256]{1,0:T(8,128)(2,1)} async-done(((bf16[832,256]{1,0:T(8,128)(2,1)}), bf16[26624,256]{1,0:T(8,128)(2,1)}) %all-gather.3.cloned.1.call-update) | async-done | bytes 13631504 | tf_op jit(solution)/shard_map/all_gather | solution.py:97
  139.2 5.4 %slice.54 = bf16[32,320,256]{2,1,0:T(8,128)(2,1)} slice(bf16[32,832,256]{2,1,0:T(8,128)(2,1)} %bitcast.142), slice={[0:32], [0:320], [0:256]} | slice | bytes 10485760 | tf_op jit(solution)/shard_map/slice | solution.py:100
  144.6 7.5 %slice_bitcast_fusion = bf16[32,256,512]{1,2,0:T(8,128)(2,1)} fusion(bf16[32,832,256]{2,1,0:T(8,128)(2,1)} %bitcast.143), kind=kLoop, calls=%fused_computation.16 | loop fusion | bytes 16777216 | tf_op jit(solution)/shard_map/qc,jcn->qjn/dot_general | solution.py:115
  152.0 12.0 %copy.26 = bf16[32,256,512]{2,1,0:T(8,128)(2,1)} copy(bf16[32,256,512]{1,2,0:T(8,128)(2,1)} %slice_bitcast_fusion) | data formatting | bytes 16777216 | tf_op jit(solution)/shard_map/qc,jcn->qjn/dot_general | solution.py:115
  164.0 2.9 fusion.62
  166.9 0.2 reverse_bitcast_fusion
  167.0 2.0 fusion.15
  169.1 0.0 copy-start.1
  169.1 6.7 %fusion.1 = (f32[4,160]{1,0:T(4,128)S(1)}, f32[5280,160,4]{0,1,2:T(8,128)}) fusion(pred[160,5280]{1,0:T(8,128)(4,1)S(1)} %get-tuple-element.27, bf16[20,4,8,128]{3,2,1,0:T(8,128)(2,1)S(1)} %get-tuple-element.20, bf16[5280,256]{1,0:T(8,128)(2,1)S(1)} %bitcast.149), kind=kOutput, calls=%fused_computation.7 | convolution fusion | flops 875212160 | bytes 15895040 | tf_op jit(solution)/shard_map/qgjd,kgd->gjqk/dot_general | solution.py:72
  175.8 9.0 %fusion.4 = f32[4,160]{1,0:T(4,128)S(1)} fusion(f32[5280,160,4]{0,1,2:T(8,128)} %get-tuple-element.24, f32[4,160]{1,0:T(4,128)S(1)} %get-tuple-element.23, pred[160,5280]{1,0:T(8,128)(4,1)S(1)} %get-tuple-element.27), kind=kLoop, calls=%fused_computation.14 | loop fusion | flops 16895360 | bytes 14366720 | tf_op jit(solution)/shard_map/reduce_sum | solution.py:78
  184.9 8.5 %fusion.24 = bf16[160,1,4,128]{3,0,2,1:T(8,128)(2,1)S(1)} fusion(bf16[5280,256]{1,0:T(8,128)(2,1)S(1)} %bitcast.150, f32[5280,160,4]{0,1,2:T(8,128)} %get-tuple-element.24, f32[4,160]{1,0:T(4,128)S(1)} %get-tuple-element.23, pred[160,5280]{1,0:T(8,128)(4,1)S(1)} %get-tuple-element.27, f32[4,160]{1,0:T(4,128)S(1)} %fusion.4), kind=kOutput, calls=%fused_computation.41 | convolution fusion | flops 882135040 | bytes 15900672 | tf_op jit(solution)/shard_map/gjqk,kgd->gjqd/dot_general | solution.py:79
  193.3 0.1 copy.25
  193.5 0.0 copy-done.1
  193.5 6.9 %fusion = (f32[4,160]{1,0:T(4,128)S(1)}, f32[5280,160,4]{0,1,2:T(8,128)}) fusion(pred[160,5280]{1,0:T(8,128)(4,1)S(1)} %get-tuple-element.28, bf16[20,4,8,128]{3,2,1,0:T(8,128)(2,1)S(1)} %get-tuple-element.19, bf16[5280,256]{1,0:T(8,128)(2,1)S(1)} %bitcast.147), kind=kOutput, calls=%fused_computation.6 | convolution fusion | flops 875212160 | bytes 15895040 | tf_op jit(solution)/shard_map/qgjd,kgd->gjqk/dot_general | solution.py:72
  200.4 0.0 slice-start
  200.4 9.2 %fusion.2 = f32[4,160]{1,0:T(4,128)S(1)} fusion(f32[5280,160,4]{0,1,2:T(8,128)} %get-tuple-element.26, f32[4,160]{1,0:T(4,128)S(1)} %get-tuple-element.25, pred[160,5280]{1,0:T(8,128)(4,1)S(1)} %get-tuple-element.28), kind=kLoop, calls=%fused_computation.12 | loop fusion | flops 16895360 | bytes 14366720 | tf_op jit(solution)/shard_map/reduce_sum | solution.py:78
  209.6 0.0 slice-start.1
  209.6 8.9 %fusion.33 = bf16[160,1,4,128]{3,0,2,1:T(8,128)(2,1)S(1)} fusion(bf16[5280,256]{1,0:T(8,128)(2,1)} %bitcast.148, f32[5280,160,4]{0,1,2:T(8,128)} %get-tuple-element.26, f32[4,160]{1,0:T(4,128)S(1)} %get-tuple-element.25, pred[160,5280]{1,0:T(8,128)(4,1)S(1)} %get-tuple-element.28, f32[4,160]{1,0:T(4,128)S(1)} %fusion.2), kind=kOutput, calls=%fused_computation.44 | convolution fusion | flops 882135040 | bytes 16128000 | tf_op jit(solution)/shard_map/gjqk,kgd->gjqd/dot_general | solution.py:79
  218.5 0.1 copy.23
  218.6 0.0 slice-done
  218.6 0.0 slice-done.1
  218.6 4.9 %convolution_convert_fusion = bf16[320,8192]{1,0:T(8,128)(2,1)} fusion(bf16[8192,512]{1,0:T(8,128)(2,1)S(1)} %bitcast.146, bf16[160,512]{1,0:T(8,128)(2,1)S(1)} %bitcast.153, bf16[160,512]{1,0:T(8,128)(2,1)S(1)} %bitcast.154), kind=kOutput, calls=%fused_computation.8 | convolution fusion | flops 2687631360 | bytes 13959168 | tf_op jit(solution)/shard_map/qc,jcn->qjn/dot_general | solution.py:115
  223.5 0.0 all-reduce.2.cloned.1.call-update
  223.5 3.8 %fusion.61 = (bf16[10240,128]{1,0:T(8,128)(2,1)}, bf16[10240,128]{1,0:T(8,128)(2,1)S(1)}) fusion(bf16[10240,256]{1,0:T(8,128)(2,1)} %bitcast.141), kind=kLoop, calls=%fused_computation.103 | loop fusion | bytes 10485760 | tf_op jit(solution)/shard_map/slice | solution.py:129
  227.3 3.8 %gather_fusion.1 = bf16[704,128]{1,0:T(8,128)(2,1)S(1)} fusion(bf16[10240,128]{1,0:T(8,128)(2,1)} %get-tuple-element.13, s32[1024]{0:T(1024)S(1)} %pad_clamp_fusion), kind=kCustom, calls=%fused_computation.1.clone | custom fusion | bytes 363264 | tf_op jit(solution)/shard_map/jit(_take)/gather | solution.py:134
  231.1 2.3 gather_fusion
  233.4 1.0 select_select_fusion
  234.4 68.0 %all-reduce.2.cloned.1.call-done = bf16[320,8192]{1,0:T(8,128)(2,1)} async-done(((bf16[320,8192]{1,0:T(8,128)(2,1)}), bf16[320,8192]{1,0:T(8,128)(2,1)}) %all-reduce.2.cloned.1.call-update) | async-done | bytes 5242896 | tf_op jit(solution)/shard_map/psum | solution.py:118
  302.5 0.0 copy-start
  302.5 6.0 %multiply_reduce_fusion = f32[320]{0:T(512)S(1)} fusion(bf16[320,8192]{1,0:T(8,128)(2,1)} %all-reduce.2.cloned.1.call-done, bf16[320,8192]{1,0:T(8,128)(2,1)} %param.13), kind=kLoop, calls=%fused_computation.10 | loop fusion | flops 13106880 | bytes 10487040 | tf_op jit(solution)/shard_map/reduce_sum | solution.py:120
  308.5 0.0 copy-done
  308.5 7.1 %multiply_convert_fusion = bf16[320,8192]{1,0:T(8,128)(2,1)} fusion(bf16[320,8192]{1,0:T(8,128)(2,1)S(1)} %copy-done, bf16[320,8192]{1,0:T(8,128)(2,1)} %param.13, f32[8192]{0:T(1024)S(1)} %convert_element_type.53, f32[320]{0:T(512)S(1)} %add_rsqrt_fusion), kind=kLoop, calls=%fused_computation.9 | loop fusion | flops 15728640 | bytes 15762688 | tf_op jit(solution)/shard_map/convert_element_type | solution.py:121
  (15 shorter events, 0.2 us)
Async XLA Ops:
  7.2 132.0 %all-gather.3.cloned.1.call-start = ((), (), s32[]{:S(2)}) async-start(), calls=%async_computation.1 | async-start | bytes 14057472 | tf_op jit(solution)/shard_map/all_gather | solution.py:97
  9.0 293.4 %all-reduce.2.cloned.1.call-start = ((), (), s32[]{:S(2)}) async-start(), calls=%async_computation | async-start | bytes 10485760 | tf_op jit(solution)/shard_map/psum | solution.py:118
  169.1 24.4 %copy-start.1 = (bf16[33,160,256]{2,1,0:T(8,128)(2,1)}, bf16[33,160,256]{2,1,0:T(8,128)(2,1)S(1)}, u32[]{:S(2)}) copy-start(bf16[33,160,256]{2,1,0:T(8,128)(2,1)S(1)} %get-tuple-element.15) | copy-start | bytes 8110084
  200.4 18.2 %slice-start = ((s8[8388608]{0:T(1024)(128)(4,1)}), s8[4194304]{0:T(1024)(128)(4,1)S(1)}, s32[]{:S(2)}) async-start(s8[8388608]{0:T(1024)(128)(4,1)} %bitcast.144), calls=%async_computation.2 | async-start | bytes 8388608
  209.6 9.0 %slice-start.1 = ((s8[8388608]{0:T(1024)(128)(4,1)}), s8[4194304]{0:T(1024)(128)(4,1)S(1)}, s32[]{:S(2)}) async-start(s8[8388608]{0:T(1024)(128)(4,1)} %bitcast.144), calls=%async_computation.3 | async-start | bytes 8388608
  302.5 6.0 %copy-start = (bf16[320,8192]{1,0:T(8,128)(2,1)S(1)}, bf16[320,8192]{1,0:T(8,128)(2,1)}, u32[]{:S(2)}) copy-start(bf16[320,8192]{1,0:T(8,128)(2,1)} %all-reduce.2.cloned.1.call-done) | copy-start | bytes 15728644
Sparse Core Ops, SparseCore 0:
  11.2 127.9 all-gather.2
  223.6 78.7 all-reduce.1
where the time goes:
time: 323 us; the launch traced here: 322 us
  waiting for transfers between devices  190 us (59%)
  other arithmetic  41.8 us (13%)
  local copies, waits for them, and re-layouts  39.9 us (12%)
  matrix products  35.9 us (11%)
  between operations  14.3 us (4%)
    all_gather x1, waiting for transfers between devices, body(): lax.all_gather(jnp.concatenate([kv_rows, out_weight], axis=0), 'seq', axi...  122 us
    psum x1, waiting for transfers between devices, body(): lax.psum(partial_value.astype(jnp.bfloat16), 'tensor').astype(jnp.float32)  68 us
    dot_general x2, local copies, waits for them, and re-layouts, body(): jnp.einsum('qc,jcn->qjn', attended, weight_blocks, preferred_element_type...  19.4 us
    reduce_sum x2, other arithmetic, attend_block(): total = jnp.sum(weights, axis=-1)  18.2 us
    dot_general x2, matrix products, attend_block(): jnp.einsum('gjqk,kgd->gjqd', weights.astype(jnp.bfloat16), value_win, pre...  17.3 us
    dot_general x2, matrix products, attend_block(): jnp.einsum('qgjd,kgd->gjqk', query_block, key_win, preferred_element_type...  13.7 us
    convert_element_type x1, other arithmetic, body(): (hidden * lax.rsqrt(mean_square + 1e-05) * norm_gain.astype(jnp.float32))...  7.13 us
  transfers between devices with their start and end apart: 2, of which 2 were waited for; matrix products, arithmetic and copies ran while one was open for 6% of the time, Pallas kernels for 0%

commit v1 on v0

--- a/solution.py
+++ b/solution.py
@@ -1,8 +1,11 @@
+import functools
 import math
 
 import jax
 import jax.numpy as jnp
 from jax import lax
+from jax.experimental import pallas as pl
+from jax.experimental.pallas import tpu as pltpu
 from jax.sharding import PartitionSpec as P
 
 HD = 128
@@ -53,68 +56,83 @@
     return (doc_start + within, is_live)
 
 
-def attend_block(query_block, block_index, kv_pos, lengths, half, kv_local, group_size, window):
-    blocks = kv_pos.shape[0]
-    start = jnp.clip(block_index - (window - 1), 0, blocks - window)
-    kv_win = lax.dynamic_slice_in_dim(kv_pos, start, window, axis=0)
-    kv_win = kv_win.reshape(window * half, -1)
-    kv_width = kv_win.shape[1] // 2
-    key_win = kv_win[:, :kv_width].reshape(window * half, kv_local, HD)
-    value_win = kv_win[:, kv_width:].reshape(window * half, kv_local, HD)
-    key_position = start * half + jnp.arange(window * half, dtype=jnp.int32)
-    query_position = block_index * half + jnp.arange(half, dtype=jnp.int32)
-    key_segment = segment_of(key_position, lengths)
-    query_segment = segment_of(query_position, lengths)
-    allowed = (key_position[None, :] <= query_position[:, None]) & (
-        key_segment[None, :] == query_segment[:, None]
-    )
-    scores = (
-        jnp.einsum("qgjd,kgd->gjqk", query_block, key_win, preferred_element_type=jnp.float32)
-        * (1.0 / math.sqrt(HD))
-    )
-    scores = jnp.where(allowed, scores, -1e30)
-    top = jnp.max(scores, axis=-1)
-    weights = jnp.where(allowed, jnp.exp(scores - top[..., None]), 0.0)
-    total = jnp.sum(weights, axis=-1)
-    accum = jnp.einsum(
-        "gjqk,kgd->gjqd",
-        weights.astype(jnp.bfloat16),
-        value_win,
-        preferred_element_type=jnp.float32,
-    )
-    return jnp.transpose(accum / total[..., None], (2, 0, 1, 3))
+def attn_kernel(q_ref, kv_ref, qpos_ref, qseg_ref, kpos_ref, kseg_ref, o_ref, *, heads, scale):
+    allowed = (kpos_ref[0] <= qpos_ref[0]) & (kseg_ref[0] == qseg_ref[0])
+    key = kv_ref[0, :, :HD]
+    value = kv_ref[0, :, HD:]
+    for h in range(heads):
+        query = q_ref[0, :, h * HD:(h + 1) * HD]
+        scores = lax.dot_general(query, key, (((1,), (1,)), ((), ())),
+                                 preferred_element_type=jnp.float32) * scale
+        scores = jnp.where(allowed, scores, -1e30)
+        top = jnp.max(scores, axis=1, keepdims=True)
+        weights = jnp.where(allowed, jnp.exp(scores - top), 0.0)
+        total = jnp.sum(weights, axis=1, keepdims=True)
+        summed = jnp.dot(weights.astype(jnp.bfloat16), value, preferred_element_type=jnp.float32)
+        o_ref[0, :, h * HD:(h + 1) * HD] = (summed / total).astype(o_ref.dtype)
 
+def attend(q, kv, qpos, qseg, kpos, kseg):
+    blocks, rows, width = q.shape
+    window = kv.shape[1]
+    heads = width // HD
+    kern = functools.partial(attn_kernel, heads=heads, scale=1.0 / math.sqrt(HD))
+    return pl.pallas_call(
+        kern,
+        grid=(blocks,),
+        in_specs=[
+            pl.BlockSpec((1, rows, width), lambda b: (b, 0, 0)),
+            pl.BlockSpec((1, window, 2 * HD), lambda b: (b, 0, 0)),
+            pl.BlockSpec((1, rows, 1), lambda b: (b, 0, 0)),
+            pl.BlockSpec((1, rows, 1), lambda b: (b, 0, 0)),
+            pl.BlockSpec((1, 1, window), lambda b: (b, 0, 0)),
+            pl.BlockSpec((1, 1, window), lambda b: (b, 0, 0)),
+        ],
+        out_specs=pl.BlockSpec((1, rows, width), lambda b: (b, 0, 0)),
+        out_shape=jax.ShapeDtypeStruct((blocks, rows, width), jnp.bfloat16),
+        compiler_params=pltpu.CompilerParams(vmem_limit_bytes=48 * 1024 * 1024),
+        cost_estimate=pl.CostEstimate(flops=4 * blocks * heads * rows * window * HD,
+                                      transcendentals=blocks * heads * rows * window,
+                                      bytes_accessed=blocks * (window * 2 * HD * 2 + 2 * rows * width * 2)),
+    )(q, kv, qpos, qseg, kpos, kseg)
 
 def body(queries, key_rows, value_rows, out_weight, residual_in, norm_gain, prompt_lengths):
     seq_count = lax.axis_size("seq")
     seq_index = lax.axis_index("seq")
     per_device = queries.shape[0]
     half = per_device // 2
-    kv_local = key_rows.shape[1] // HD
-    group_size = queries.shape[1] // (kv_local * HD)
     kv_width = key_rows.shape[1]
     kv_rows = jnp.concatenate([key_rows, value_rows], axis=1)
     stacked = lax.all_gather(
-        jnp.concatenate([kv_rows, out_weight], axis=0), "seq", axis=0, tiled=False
+        jnp.concatenate([kv_rows, out_weight], axis=0), "seq", axis=1, tiled=True
     )
-    kv_piece = stacked[:, :per_device].reshape(seq_count * per_device, 2 * kv_width)
-    weight_blocks = stacked[:, per_device:]
-    halves = kv_piece.reshape(seq_count, 2, half, 2 * kv_width)
-    kv_pos = jnp.concatenate([halves[:, 0], halves[::-1, 1]], axis=0)
-    window = min(2 * seq_count, (MAX_PROMPT - 1 + half - 1) // half + 1)
-    grouped = queries.reshape(2, half, kv_local, group_size, HD)
-    first = attend_block(
-        grouped[0], seq_index, kv_pos, prompt_lengths, half, kv_local, group_size, window
+    weight_full = stacked[per_device:]
+    kv_stored = jnp.transpose(
+        stacked[:per_device].reshape(per_device, seq_count, 2 * kv_width), (1, 0, 2)
     )
-    second = attend_block(
-        grouped[1], 2 * seq_count - 1 - seq_index, kv_pos, prompt_lengths, half, kv_local,
-        group_size, window,
+    kv_piece = kv_stored.reshape(seq_count * per_device, 2 * kv_width)
+    halves = kv_stored.reshape(seq_count, 2, half, 2 * kv_width)
+    kv_pos = jnp.concatenate([halves[:, 0], halves[::-1, 1]], axis=0).reshape(
+        seq_count * per_device, 2 * kv_width
     )
-    attended = jnp.concatenate([first, second], axis=0)
-    attended = attended.reshape(per_device, -1).astype(jnp.bfloat16)
-    partial_value = jnp.einsum(
-        "qc,jcn->qjn", attended, weight_blocks, preferred_element_type=jnp.float32
+    window = min(seq_count * per_device, -(-(MAX_PROMPT - 1 + half) // 128) * 128)
+    block_index = jnp.stack([seq_index, 2 * seq_count - 1 - seq_index])
+    starts = jnp.clip(block_index * half + half - window, 0, seq_count * per_device - window)
+    kv_win = jnp.stack(
+        [lax.dynamic_slice_in_dim(kv_pos, starts[i], window, axis=0) for i in range(2)]
+    )
+    key_position = starts[:, None] + jnp.arange(window, dtype=jnp.int32)[None, :]
+    query_position = block_index[:, None] * half + jnp.arange(half, dtype=jnp.int32)[None, :]
+    key_segment = segment_of(key_position.reshape(-1), prompt_lengths).reshape(2, 1, window)
+    query_segment = segment_of(query_position.reshape(-1), prompt_lengths).reshape(2, half, 1)
+    attended = attend(
+        queries.reshape(2, half, queries.shape[1]),
+        kv_win,
+        query_position[:, :, None],
+        query_segment,
+        key_position[:, None, :],
+        key_segment,
     ).reshape(per_device, -1)
+    partial_value = jnp.dot(attended, weight_full, preferred_element_type=jnp.float32)
     projected = lax.psum(partial_value.astype(jnp.bfloat16), "tensor").astype(jnp.float32)
     hidden = residual_in.astype(jnp.float32) + projected
     mean_square = jnp.mean(hidden * hidden, axis=-1, keepdims=True)

time: 323 us -> 286 us (0.89)
  matrix products: 35.9 us -> 8.63 us
  other arithmetic: 41.8 us -> 23.8 us
  Pallas kernels: 0 us -> 17.2 us
  local copies, waits for them, and re-layouts: 39.9 us -> 22.9 us
  waiting for transfers between devices: 190 us -> 195 us
  between operations: 14.3 us -> 17.9 us
    dot_general x5 -> x1, matrix products: 35.9 us -> 8.63 us  [body(): jnp.dot(attended, weight_full, preferred_element_type=jnp.float32)]
    dot_general x2 -> x0, local copies, waits for them, and re-layouts: 19.4 us -> none  [body(): jnp.einsum('qc,jcn->qjn', attended, weight_blocks, preferred_element_type...]
    reduce_sum x2 -> x0, other arithmetic: 18.2 us -> none  [attend_block(): total = jnp.sum(weights, axis=-1)]
    pallas_call x0 -> x1, Pallas kernels: none -> 17.2 us  [attend(): pl.pallas_call(kern, grid=(blocks,), in_specs=[pl.BlockSpec((1, rows, wid...]
    slice x2 -> x3, local copies, waits for them, and re-layouts: 8.27 us -> 3.99 us  [the longest x1 2.82 us: body(): stacked[:per_device].reshape(per_device, seq_count, 2 * kv_width)]
    all_gather x1, waiting for transfers between devices: 122 us -> 126 us  [body(): lax.all_gather(jnp.concatenate([kv_rows, out_weight], axis=0), 'seq', axi...]
    reshape x0 -> x3, local copies, waits for them, and re-layouts: none -> 3.37 us  [the longest x1 3.12 us: body(): stacked[:per_device].reshape(per_device, seq_count, 2 * kv_width)]
where the time goes in v1:
time: 286 us
  waiting for transfers between devices  195 us (68%)
  other arithmetic  23.8 us (8%)
  local copies, waits for them, and re-layouts  22.9 us (8%)
  between operations  17.9 us (6%)
  Pallas kernels  17.2 us (6%)
  matrix products  8.63 us (3%)
    all_gather x1, waiting for transfers between devices, body(): lax.all_gather(jnp.concatenate([kv_rows, out_weight], axis=0), 'seq', axi...  126 us
    psum x1, waiting for transfers between devices, body(): lax.psum(partial_value.astype(jnp.bfloat16), 'tensor').astype(jnp.float32)  68.8 us
    pallas_call x1, Pallas kernels, attend(): pl.pallas_call(kern, grid=(blocks,), in_specs=[pl.BlockSpec((1, rows, wid...  17.2 us
    dot_general x1, matrix products, body(): jnp.dot(attended, weight_full, preferred_element_type=jnp.float32)  8.63 us
    convert_element_type x1, other arithmetic, body(): (hidden * lax.rsqrt(mean_square + 1e-05) * norm_gain.astype(jnp.float32))...  7.13 us
    reduce_sum x1, other arithmetic, body(): mean_square = jnp.mean(hidden * hidden, axis=-1, keepdims=True)  5.99 us
  transfers between devices with their start and end apart: 2, of which 2 were waited for; matrix products, arithmetic and copies ran while one was open for 6% of the time, Pallas kernels for 0%

profile of v1, /device:TPU:1, one launch (start us, length us, event | category | flops | bytes accessed | tf_op | source)
XLA Modules:
  0.0 285.6 jit_solution(8133191150829597179)
XLA Ops:
  7.2 0.0 all-gather.2.cloned.1.call-start
  7.2 1.8 pad_maximum_fusion.2
  9.0 0.0 all-gather.2.cloned.1.call-update
  9.0 0.0 all-reduce.2.cloned.1.call-start
  9.1 0.1 add_clamp_fusion
  9.2 0.6 fusion.14
  12.2 0.1 iota_add_fusion.1
  12.3 0.7 copy.24
  13.1 0.1 reduce
  13.2 0.3 convert_reduce_fusion
  13.5 0.1 iota_add_fusion.4
  13.6 0.1 add.167
  13.7 0.1 convert_reduce_fusion.1
  13.8 0.2 reshape.283.qseg_ref
  14.0 0.7 convert_element_type.32
  14.7 0.7 fusion.17
  15.4 0.1 copy.26
  15.5 0.1 reduce.1
  16.9 0.7 fusion.10
  17.6 0.7 fusion.16
  18.2 0.8 fusion.4
  19.1 0.1 iota_add_fusion.qpos_ref
  19.2 0.1 iota_add_fusion.2.kpos_ref
  19.3 126.3 %all-gather.2.cloned.1.call-done = bf16[832,8192]{1,0:T(8,128)(2,1)} async-done(((bf16[832,256]{1,0:T(8,128)(2,1)}), bf16[832,8192]{1,0:T(8,128)(2,1)}) %all-gather.2.cloned.1.call-update) | async-done | bytes 13631504 | tf_op jit(solution)/shard_map/all_gather | solution.py:105
  145.5 2.8 slice.36
  148.4 0.0 copy-start.1
  148.4 1.8 copy.32
  150.2 0.5 copy-done.1
  150.7 0.6 fusion.13
  151.2 1.5 copy.30
  152.8 1.6 copy_bitcast_fusion.1
  154.3 0.5 pad_maximum_fusion.1
  154.8 1.4 dynamic-slice_bitcast_fusion.1
  156.2 0.0 copy-start
  156.2 2.8 pad_maximum_fusion.kv_ref
  159.0 0.0 copy-done
  159.0 17.2 %shard_map.94 = bf16[2,160,512]{2,1,0:T(8,128)(2,1)S(1)} custom-call(bf16[2,160,512]{2,1,0:T(8,128)(2,1)S(1)} %bitcast.33, bf16[2,5376,256]{2,1,0:T(8,128)(2,1)} %pad_maximum_fusion.kv_ref, s32[2,160,1]{2,1,0:T(8,128)S(1)} %iota_add_fusion.qpos_ref, s32[2,160,1]{2,1,0:T(8,128)S(1)} %reshape.283.qseg_ref, s32[2,1,5376]{2,1,0:T(1,128)S(1)} %iota_add_fusion.2.kpos_ref, ...), custom_call_target="tpu_custom_call" | custom-call | flops 3523215360 | bytes 6160384 | tf_op jit(solution)/shard_map/pallas_call | solution.py:79
  176.3 8.6 %convolution_convert_fusion = bf16[320,8192]{1,0:T(8,128)(2,1)} fusion(bf16[320,512]{1,0:T(8,128)(2,1)S(1)} %bitcast.34, bf16[832,8192]{1,0:T(8,128)(2,1)} %all-gather.2.cloned.1.call-done), kind=kOutput, calls=%fused_computation.2 | convolution fusion | flops 2686976000 | bytes 13959168 | tf_op jit(solution)/shard_map/dot_general | solution.py:135
  184.9 0.0 all-reduce.2.cloned.1.call-update
  184.9 3.1 %copy.35 = bf16[40,32,8,256]{3,2,0,1:T(8,128)(2,1)S(1)} copy(bf16[40,32,8,256]{3,2,1,0:T(8,128)(2,1)} %bitcast.36) | data formatting | bytes 10485760 | tf_op jit(solution)/shard_map/reshape | solution.py:110
  188.1 1.7 fusion.12
  189.8 3.8 %gather_fusion = bf16[704,128]{1,0:T(8,128)(2,1)S(1)} fusion(bf16[10240,128]{1,0:T(8,128)(2,1)} %get-tuple-element.12, s32[1024]{0:T(1024)S(1)} %pad_clamp_fusion), kind=kCustom, calls=%fused_computation.clone | custom fusion | bytes 363264 | tf_op jit(solution)/shard_map/jit(_take)/gather | solution.py:151
  193.6 2.2 gather_fusion.1
  195.8 1.0 select_select_fusion
  196.8 68.8 %all-reduce.2.cloned.1.call-done = bf16[320,8192]{1,0:T(8,128)(2,1)} async-done(((bf16[320,8192]{1,0:T(8,128)(2,1)}), bf16[320,8192]{1,0:T(8,128)(2,1)}) %all-reduce.2.cloned.1.call-update) | async-done | bytes 5242896 | tf_op jit(solution)/shard_map/psum | solution.py:136
  265.7 0.0 copy-start.2
  265.7 6.0 %multiply_reduce_fusion = f32[320]{0:T(512)S(1)} fusion(bf16[320,8192]{1,0:T(8,128)(2,1)} %all-reduce.2.cloned.1.call-done, bf16[320,8192]{1,0:T(8,128)(2,1)} %param.13), kind=kLoop, calls=%fused_computation.4 | loop fusion | flops 13106880 | bytes 10487040 | tf_op jit(solution)/shard_map/reduce_sum | solution.py:138
  271.7 0.0 copy-done.2
  271.7 7.1 %multiply_convert_fusion = bf16[320,8192]{1,0:T(8,128)(2,1)} fusion(bf16[320,8192]{1,0:T(8,128)(2,1)S(1)} %copy-done.2, bf16[320,8192]{1,0:T(8,128)(2,1)} %param.13, f32[8192]{0:T(1024)S(1)} %convert_element_type.32, f32[320]{0:T(512)S(1)} %add_rsqrt_fusion), kind=kLoop, calls=%fused_computation.3 | loop fusion | flops 15728640 | bytes 15762688 | tf_op jit(solution)/shard_map/convert_element_type | solution.py:139
  (10 shorter events, 0.2 us)
Async XLA Ops:
  7.2 138.4 %all-gather.2.cloned.1.call-start = ((), (), s32[]{:S(2)}) async-start(), calls=%async_computation | async-start | bytes 14057472 | tf_op jit(solution)/shard_map/all_gather | solution.py:105
  9.0 256.6 %all-reduce.2.cloned.1.call-start = ((), (), s32[]{:S(2)}) async-start(), calls=%async_computation.1 | async-start | bytes 10485760 | tf_op jit(solution)/shard_map/psum | solution.py:136
  148.4 2.3 copy-start.1
  156.2 2.8 copy-start
  265.7 6.0 %copy-start.2 = (bf16[320,8192]{1,0:T(8,128)(2,1)S(1)}, bf16[320,8192]{1,0:T(8,128)(2,1)}, u32[]{:S(2)}) copy-start(bf16[320,8192]{1,0:T(8,128)(2,1)} %all-reduce.2.cloned.1.call-done) | copy-start | bytes 15728644
Sparse Core Ops, SparseCore 0:
  11.0 134.4 all-gather.1
  185.1 80.5 all-reduce.1

commit v2 on v1

--- a/solution.py
+++ b/solution.py
@@ -95,6 +95,33 @@
                                       bytes_accessed=blocks * (window * 2 * HD * 2 + 2 * rows * width * 2)),
     )(q, kv, qpos, qseg, kpos, kseg)
 
+def norm_kernel(projected_ref, residual_ref, gain_ref, out_ref):
+    hidden = residual_ref[...].astype(jnp.float32) + projected_ref[...].astype(jnp.float32)
+    mean_square = jnp.mean(hidden * hidden, axis=-1, keepdims=True)
+    out_ref[...] = (
+        hidden * lax.rsqrt(mean_square + 1e-05) * gain_ref[...].astype(jnp.float32)
+    ).astype(out_ref.dtype)
+
+
+def residual_norm(projected, residual, gain, rows_per_step=40):
+    rows, width = projected.shape
+    steps = rows // rows_per_step
+    return pl.pallas_call(
+        norm_kernel,
+        grid=(steps,),
+        in_specs=[
+            pl.BlockSpec((rows_per_step, width), lambda i: (i, 0)),
+            pl.BlockSpec((rows_per_step, width), lambda i: (i, 0)),
+            pl.BlockSpec((1, width), lambda i: (0, 0)),
+        ],
+        out_specs=pl.BlockSpec((rows_per_step, width), lambda i: (i, 0)),
+        out_shape=jax.ShapeDtypeStruct((rows, width), jnp.bfloat16),
+        cost_estimate=pl.CostEstimate(
+            flops=5 * rows * width, transcendentals=rows, bytes_accessed=6 * rows * width
+        ),
+    )(projected, residual, gain.reshape(1, width))
+
+
 def body(queries, key_rows, value_rows, out_weight, residual_in, norm_gain, prompt_lengths):
     seq_count = lax.axis_size("seq")
     seq_index = lax.axis_index("seq")
@@ -133,12 +160,8 @@
         key_segment,
     ).reshape(per_device, -1)
     partial_value = jnp.dot(attended, weight_full, preferred_element_type=jnp.float32)
-    projected = lax.psum(partial_value.astype(jnp.bfloat16), "tensor").astype(jnp.float32)
-    hidden = residual_in.astype(jnp.float32) + projected
-    mean_square = jnp.mean(hidden * hidden, axis=-1, keepdims=True)
-    normed = (hidden * lax.rsqrt(mean_square + 1e-05) * norm_gain.astype(jnp.float32)).astype(
-        jnp.bfloat16
-    )
+    projected = lax.psum(partial_value.astype(jnp.bfloat16), "tensor")
+    normed = residual_norm(projected, residual_in, norm_gain)
     slot_ids = seq_index * SLOT_DEV + jnp.arange(SLOT_DEV, dtype=jnp.int32)
     source, is_live = slot_source(slot_ids, prompt_lengths, PAGE)
     target = stored_row(source, per_device, seq_count)

time: 286 us -> 283 us (0.990)
  other arithmetic: 23.8 us -> 9.96 us
  Pallas kernels: 17.2 us -> 27.2 us
    pallas_call x0 -> x1, Pallas kernels: none -> 9.99 us  [residual_norm(): pl.pallas_call(norm_kernel, grid=(steps,), in_specs=[pl.BlockSpec((rows_p...]
    convert_element_type x2 -> x0, other arithmetic: 7.85 us -> none  [the longest x1 7.13 us: body(): (hidden * lax.rsqrt(mean_square + 1e-05) * norm_gain.astype(jnp.float32))...]
    reduce_sum x1 -> x0, other arithmetic: 5.99 us -> none  [body(): mean_square = jnp.mean(hidden * hidden, axis=-1, keepdims=True)]
  transfers between devices with their start and end apart: 2 -> 2, of which waited for: 2 -> 2; matrix products, arithmetic and copies ran while one was open for 6% -> 7% of each run, Pallas kernels for 0% -> 0%
where the time goes in v2:
time: 283 us; the launch traced here: 282 us
  waiting for transfers between devices  195 us (69%)
  Pallas kernels  27.2 us (10%)
  local copies, waits for them, and re-layouts  24 us (8%)
  between operations  17.9 us (6%)
  other arithmetic  9.96 us (4%)
  matrix products  8.63 us (3%)
    all_gather x1, waiting for transfers between devices, body(): lax.all_gather(jnp.concatenate([kv_rows, out_weight], axis=0), 'seq', axi...  126 us
    psum x1, waiting for transfers between devices, body(): projected = lax.psum(partial_value.astype(jnp.bfloat16), 'tensor')  69 us
    pallas_call x1, Pallas kernels, attend(): pl.pallas_call(kern, grid=(blocks,), in_specs=[pl.BlockSpec((1, rows, wid...  17.2 us
    pallas_call x1, Pallas kernels, residual_norm(): pl.pallas_call(norm_kernel, grid=(steps,), in_specs=[pl.BlockSpec((rows_p...  9.99 us
    dot_general x1, matrix products, body(): jnp.dot(attended, weight_full, preferred_element_type=jnp.float32)  8.63 us
  transfers between devices with their start and end apart: 2, of which 2 were waited for; matrix products, arithmetic and copies ran while one was open for 7% of the time, Pallas kernels for 0%

profile of v2, /device:TPU:1, one launch (start us, length us, event | category | flops | bytes accessed | tf_op | source)
XLA Modules:
  0.0 282.5 jit_solution(12787977935497382837)
XLA Ops:
  7.2 0.0 all-gather.2.cloned.1.call-start
  7.2 1.8 pad_maximum_fusion.2
  9.0 0.0 all-gather.2.cloned.1.call-update
  9.0 0.0 all-reduce.2.cloned.1.call-start
  9.1 0.1 add_clamp_fusion
  9.2 0.6 fusion.14
  12.2 0.1 iota_add_fusion.1
  12.3 0.7 copy.24
  13.1 0.1 reduce
  13.2 0.3 convert_reduce_fusion
  13.5 0.1 iota_add_fusion.4
  13.6 0.1 add.153
  13.7 0.1 convert_reduce_fusion.1
  13.8 0.2 reshape.278.qseg_ref
  14.0 1.3 reshape.252.gain_ref
  15.3 0.7 fusion.17
  16.0 0.1 copy.26
  16.1 0.1 reduce.1
  17.5 0.7 fusion.10
  18.2 0.7 fusion.16
  18.8 0.8 fusion.4
  19.7 0.1 iota_add_fusion.qpos_ref
  19.8 0.1 iota_add_fusion.2.kpos_ref
  19.9 125.7 %all-gather.2.cloned.1.call-done = bf16[832,8192]{1,0:T(8,128)(2,1)} async-done(((bf16[832,256]{1,0:T(8,128)(2,1)}), bf16[832,8192]{1,0:T(8,128)(2,1)}) %all-gather.2.cloned.1.call-update) | async-done | bytes 13631504 | tf_op jit(solution)/shard_map/all_gather | solution.py:132
  145.5 2.8 slice.36
  148.4 0.0 copy-start.1
  148.4 1.8 copy.32
  150.2 0.5 copy-done.1
  150.7 0.6 fusion.13
  151.2 1.5 copy.30
  152.8 1.6 copy_bitcast_fusion.1
  154.3 0.5 pad_maximum_fusion.1
  154.8 1.4 dynamic-slice_bitcast_fusion.1
  156.2 0.0 copy-start
  156.2 2.8 %pad_maximum_fusion.kv_ref = bf16[2,5376,256]{2,1,0:T(8,128)(2,1)} fusion(bf16[1,5376,256]{2,1,0:T(8,128)(2,1)S(1)} %get-tuple-element.14, bf16[1,5376,256]{2,1,0:T(8,128)(2,1)S(1)} %get-tuple-element.13), kind=kLoop, calls=%fused_computation.4 | loop fusion | flops 2752512 | bytes 11010048 | tf_op jit(solution)/shard_map/stack | solution.py:147
  159.0 0.0 copy-done
  159.0 17.2 %shard_map.94 = bf16[2,160,512]{2,1,0:T(8,128)(2,1)S(1)} custom-call(bf16[2,160,512]{2,1,0:T(8,128)(2,1)S(1)} %bitcast.33, bf16[2,5376,256]{2,1,0:T(8,128)(2,1)} %pad_maximum_fusion.kv_ref, s32[2,160,1]{2,1,0:T(8,128)S(1)} %iota_add_fusion.qpos_ref, s32[2,160,1]{2,1,0:T(8,128)S(1)} %reshape.278.qseg_ref, s32[2,1,5376]{2,1,0:T(1,128)S(1)} %iota_add_fusion.2.kpos_ref, ...), custom_call_target="tpu_custom_call" | custom-call | flops 3523215360 | bytes 6160384 | tf_op jit(solution)/shard_map/pallas_call | solution.py:79
  176.3 8.6 %convolution_convert_fusion = bf16[320,8192]{1,0:T(8,128)(2,1)} fusion(bf16[320,512]{1,0:T(8,128)(2,1)S(1)} %bitcast.34, bf16[832,8192]{1,0:T(8,128)(2,1)} %all-gather.2.cloned.1.call-done), kind=kOutput, calls=%fused_computation.2 | convolution fusion | flops 2686976000 | bytes 13959168 | tf_op jit(solution)/shard_map/dot_general | solution.py:162
  184.9 0.0 all-reduce.2.cloned.1.call-update
  184.9 3.1 %copy.35 = bf16[40,32,8,256]{3,2,0,1:T(8,128)(2,1)S(1)} copy(bf16[40,32,8,256]{3,2,1,0:T(8,128)(2,1)} %bitcast.36) | data formatting | bytes 10485760 | tf_op jit(solution)/shard_map/reshape | solution.py:137
  188.1 1.7 fusion.12
  189.8 3.8 %gather_fusion = bf16[704,128]{1,0:T(8,128)(2,1)S(1)} fusion(bf16[10240,128]{1,0:T(8,128)(2,1)} %get-tuple-element.12, s32[1024]{0:T(1024)S(1)} %pad_clamp_fusion), kind=kCustom, calls=%fused_computation.clone | custom fusion | bytes 363264 | tf_op jit(solution)/shard_map/jit(_take)/gather | solution.py:174
  193.6 2.0 gather_fusion.1
  195.6 1.0 select_select_fusion
  196.6 69.0 %all-reduce.2.cloned.1.call-done.projected_ref = bf16[320,8192]{1,0:T(8,128)(2,1)} async-done(((bf16[320,8192]{1,0:T(8,128)(2,1)}), bf16[320,8192]{1,0:T(8,128)(2,1)}) %all-reduce.2.cloned.1.call-update) | async-done | bytes 5242896 | tf_op jit(solution)/shard_map/psum | solution.py:163
  265.7 10.0 %shard_map.95 = bf16[320,8192]{1,0:T(8,128)(2,1)} custom-call(bf16[320,8192]{1,0:T(8,128)(2,1)} %all-reduce.2.cloned.1.call-done.projected_ref, bf16[320,8192]{1,0:T(8,128)(2,1)} %residual_ref.1, bf16[1,8192]{1,0:T(2,128)(2,1)} %reshape.252.gain_ref), custom_call_target="tpu_custom_call" | custom-call | flops 13107200 | bytes 15728640 | tf_op jit(solution)/shard_map/pallas_call | solution.py:109
  (9 shorter events, 0.2 us)
Async XLA Ops:
  7.2 138.4 %all-gather.2.cloned.1.call-start = ((), (), s32[]{:S(2)}) async-start(), calls=%async_computation | async-start | bytes 14057472 | tf_op jit(solution)/shard_map/all_gather | solution.py:132
  9.0 256.6 %all-reduce.2.cloned.1.call-start = ((), (), s32[]{:S(2)}) async-start(), calls=%async_computation.1 | async-start | bytes 10485760 | tf_op jit(solution)/shard_map/psum | solution.py:163
  148.4 2.3 copy-start.1
  156.2 2.8 %copy-start = (bf16[320,512]{1,0:T(8,128)(2,1)S(1)}, bf16[320,512]{1,0:T(8,128)(2,1)}, u32[]{:S(2)}) copy-start(bf16[320,512]{1,0:T(8,128)(2,1)} %param.9) | copy-start | bytes 983044
Sparse Core Ops, SparseCore 0:
  11.0 134.4 all-gather.1
  185.1 80.5 all-reduce.1

commit v3 on v2

--- a/solution.py
+++ b/solution.py
@@ -122,6 +122,21 @@
     )(projected, residual, gain.reshape(1, width))
 
 
+def pair_then_ring_sum(partial):
+    half_cols = partial.shape[1] // 2
+    core = lax.axis_index("tc")
+    swap = [(0, 1), (1, 0)]
+    mine = lax.dynamic_slice_in_dim(partial, core * half_cols, half_cols, axis=1)
+    other = lax.dynamic_slice_in_dim(partial, (1 - core) * half_cols, half_cols, axis=1)
+    received = lax.ppermute(other, "tc", swap)
+    pair = (mine.astype(jnp.float32) + received.astype(jnp.float32)).astype(jnp.bfloat16)
+    reduced = lax.psum(pair, "ty")
+    partner = lax.ppermute(reduced, "tc", swap)
+    first = jnp.where(core == 0, reduced, partner)
+    second = jnp.where(core == 0, partner, reduced)
+    return jnp.concatenate([first, second], axis=1)
+
+
 def body(queries, key_rows, value_rows, out_weight, residual_in, norm_gain, prompt_lengths):
     seq_count = lax.axis_size("seq")
     seq_index = lax.axis_index("seq")
@@ -160,7 +175,7 @@
         key_segment,
     ).reshape(per_device, -1)
     partial_value = jnp.dot(attended, weight_full, preferred_element_type=jnp.float32)
-    projected = lax.psum(partial_value.astype(jnp.bfloat16), "tensor")
+    projected = pair_then_ring_sum(partial_value.astype(jnp.bfloat16))
     normed = residual_norm(projected, residual_in, norm_gain)
     slot_ids = seq_index * SLOT_DEV + jnp.arange(SLOT_DEV, dtype=jnp.int32)
     source, is_live = slot_source(slot_ids, prompt_lengths, PAGE)
@@ -177,18 +192,23 @@
 
 
 def solution(mesh):
+    seq_count, tensor_count = mesh.devices.shape
+    split = jax.sharding.Mesh(
+        mesh.devices.reshape(seq_count, tensor_count // 2, 2), ("seq", "ty", "tc")
+    )
+    tensor = ("ty", "tc")
     return jax.shard_map(
         body,
-        mesh=mesh,
+        mesh=split,
         in_specs=(
-            P("seq", "tensor"),
-            P("seq", "tensor"),
-            P("seq", "tensor"),
-            P("tensor", "seq"),
+            P("seq", tensor),
+            P("seq", tensor),
+            P("seq", tensor),
+            P(tensor, "seq"),
             P("seq", None),
             P(),
             P(),
         ),
-        out_specs=(P("seq", None), P("seq", "tensor"), P("seq", "tensor")),
+        out_specs=(P("seq", None), P("seq", tensor), P("seq", tensor)),
         check_vma=False,
     )

time: 283 us -> 302 us (1.067)
  local copies, waits for them, and re-layouts: 24 us -> 31.7 us
  other arithmetic: 9.96 us -> 17.1 us
  starting transfers between devices: 0.08 us -> 3.89 us
    psum x1, waiting for transfers between devices: 69 us -> 62.5 us  [pair_then_ring_sum(): reduced = lax.psum(pair, 'ty')]
    ppermute x0 -> x2, waiting for transfers between devices: none -> 4.75 us  [the longest x1 4.74 us: pair_then_ring_sum(): received = lax.ppermute(other, 'tc', swap)]
    all_gather x1, waiting for transfers between devices: 126 us -> 130 us  [body(): lax.all_gather(jnp.concatenate([kv_rows, out_weight], axis=0), 'seq', axi...]
    convert_element_type x0 -> x1, other arithmetic: none -> 4.24 us  [pair_then_ring_sum(): (mine.astype(jnp.float32) + received.astype(jnp.float32)).astype(jnp.bflo...]
    ppermute x0 -> x2, starting transfers between devices: none -> 3.81 us  [the longest x1 3.13 us: pair_then_ring_sum(): received = lax.ppermute(other, 'tc', swap)]
    unnamed x6 -> x12, local copies, waits for them, and re-layouts: 3.8 us -> 6.14 us
  transfers between devices with their start and end apart: 2 -> 4, of which waited for: 2 -> 3; matrix products, arithmetic and copies ran while one was open for 7% -> 7% of each run, Pallas kernels for 0% -> 0%
where the time goes in v3:
time: 302 us
  waiting for transfers between devices  197 us (65%)
  local copies, waits for them, and re-layouts  31.7 us (10%)
  Pallas kernels  27.3 us (9%)
  between operations  17.9 us (6%)
  other arithmetic  17.1 us (6%)
  matrix products  6.43 us (2%)
  starting transfers between devices  3.89 us (1%)
    all_gather x1, waiting for transfers between devices, body(): lax.all_gather(jnp.concatenate([kv_rows, out_weight], axis=0), 'seq', axi...  130 us
    psum x1, waiting for transfers between devices, pair_then_ring_sum(): reduced = lax.psum(pair, 'ty')  62.5 us
    pallas_call x1, Pallas kernels, attend(): pl.pallas_call(kern, grid=(blocks,), in_specs=[pl.BlockSpec((1, rows, wid...  17.3 us
    pallas_call x1, Pallas kernels, residual_norm(): pl.pallas_call(norm_kernel, grid=(steps,), in_specs=[pl.BlockSpec((rows_p...  9.99 us
    dot_general x1, matrix products, body(): jnp.dot(attended, weight_full, preferred_element_type=jnp.float32)  6.43 us
    unnamed x12, local copies, waits for them, and re-layouts  6.14 us
  transfers between devices with their start and end apart: 4, of which 3 were waited for; matrix products, arithmetic and copies ran while one was open for 7% of the time, Pallas kernels for 0%

profile of v3, /device:TPU:1, one launch (start us, length us, event | category | flops | bytes accessed | tf_op | source)
XLA Modules:
  0.0 301.7 jit_solution(2065783731133816754)
XLA Ops:
  7.2 0.0 all-gather.2.cloned.1.call-start
  7.2 1.8 pad_maximum_fusion.3
  9.0 0.0 all-gather.2.cloned.1.call-update
  9.0 0.0 all-reduce.2.cloned.1.call-start
  9.1 0.1 add_clamp_fusion
  9.2 0.6 fusion.14
  12.2 0.1 iota_add_fusion.1
  12.3 0.7 copy.24
  13.1 0.1 reduce
  13.2 0.3 convert_reduce_fusion
  13.5 0.1 iota_add_fusion.4
  13.6 0.1 add.162
  13.7 0.1 convert_reduce_fusion.1
  13.8 0.2 reshape.278.qseg_ref
  15.2 0.1 iota_add_fusion.qpos_ref
  15.3 0.1 iota_add_fusion.2.kpos_ref
  15.4 130.1 %all-gather.2.cloned.1.call-done = bf16[832,8192]{1,0:T(8,128)(2,1)} async-done(((bf16[832,256]{1,0:T(8,128)(2,1)}), bf16[832,8192]{1,0:T(8,128)(2,1)}) %all-gather.2.cloned.1.call-update) | async-done | bytes 13631504 | tf_op jit(solution)/shard_map/all_gather | solution.py:147
  145.5 2.8 slice.36
  148.4 0.0 copy-start.1
  148.4 1.8 copy.32
  150.2 0.5 copy-done.1
  150.7 0.6 fusion.13
  151.2 1.5 copy.30
  152.7 1.6 copy_bitcast_fusion.1
  154.3 0.5 pad_maximum_fusion.1
  154.8 1.3 dynamic-slice_bitcast_fusion.1
  156.1 0.0 copy-start
  156.1 2.8 pad_maximum_fusion.kv_ref
  158.9 0.0 copy-done
  158.9 17.3 %shard_map.94 = bf16[2,160,512]{2,1,0:T(8,128)(2,1)S(1)} custom-call(bf16[2,160,512]{2,1,0:T(8,128)(2,1)S(1)} %bitcast.33, bf16[2,5376,256]{2,1,0:T(8,128)(2,1)} %pad_maximum_fusion.kv_ref, s32[2,160,1]{2,1,0:T(8,128)S(1)} %iota_add_fusion.qpos_ref, s32[2,160,1]{2,1,0:T(8,128)S(1)} %reshape.278.qseg_ref, s32[2,1,5376]{2,1,0:T(1,128)S(1)} %iota_add_fusion.2.kpos_ref, ...), custom_call_target="tpu_custom_call" | custom-call | flops 3523215360 | bytes 6160384 | tf_op jit(solution)/shard_map/pallas_call | solution.py:79
  176.2 6.4 %convolution_convert_fusion = bf16[320,8192]{1,0:T(8,128)(2,1)S(1)} fusion(bf16[320,512]{1,0:T(8,128)(2,1)S(1)} %bitcast.34, bf16[832,8192]{1,0:T(8,128)(2,1)} %all-gather.2.cloned.1.call-done), kind=kOutput, calls=%fused_computation.2 | convolution fusion | flops 2686976000 | bytes 13959168 | tf_op jit(solution)/shard_map/dot_general | solution.py:177
  182.7 0.0 copy-start.2
  182.7 2.3 copy-done.2
  185.0 1.8 constant_dynamic-slice_fusion
  186.8 3.1 %collective-permute-start = (bf16[320,4096]{1,0:T(8,128)(2,1)}, bf16[320,4096]{1,0:T(8,128)(2,1)S(1)}, u32[]{:S(2)}, u32[]{:S(2)}) collective-permute-start(bf16[320,4096]{1,0:T(8,128)(2,1)} %constant_dynamic-slice_fusion), channel_id=1, source_target_pairs={{0,1},{1,0},{2,3},{3,2},{4,5},{5,4},{6,7},{7,6},{8,9},{9,8},{10,11... | collective-permute-start | bytes 7864328 | tf_op jit(solution)/shard_map/ppermute | solution.py:131
  190.0 0.0 copy-start.3
  190.0 0.0 copy-start.4
  190.0 4.7 %collective-permute-done = bf16[320,4096]{1,0:T(8,128)(2,1)S(1)} collective-permute-done((bf16[320,4096]{1,0:T(8,128)(2,1)}, bf16[320,4096]{1,0:T(8,128)(2,1)S(1)}, u32[]{:S(2)}, u32[]{:S(2)}) %collective-permute-start) | collective-permute-done | bytes 2621472 | tf_op jit(solution)/shard_map/ppermute | solution.py:131
  194.7 4.2 %add_convert_fusion = bf16[320,4096]{1,0:T(8,128)(2,1)} fusion(bf16[320,4096]{1,0:T(8,128)(2,1)S(1)} %collective-permute-done, bf16[320,8192]{1,0:T(8,128)(2,1)} %copy-done.2, s32[]{:T(128)S(6)} %select_n.80), kind=kLoop, calls=%fused_computation.8 | loop fusion | flops 5242880 | bytes 7864324 | tf_op jit(solution)/shard_map/convert_element_type | solution.py:132
  199.0 0.0 all-reduce.2.cloned.1.call-update
  199.0 0.0 copy-done.3
  199.0 0.6 reshape.252.gain_ref
  199.6 0.0 copy-done.4
  199.6 0.1 copy.26
  199.8 0.1 reduce.1
  199.9 0.1 fusion.4
  200.1 5.5 %copy.35 = bf16[40,32,8,256]{3,2,0,1:T(8,128)(2,1)} copy(bf16[40,32,8,256]{3,2,1,0:T(8,128)(2,1)} %bitcast.36) | data formatting | bytes 10485760 | tf_op jit(solution)/shard_map/reshape | solution.py:152
  205.6 62.5 %all-reduce.2.cloned.1.call-done = bf16[320,4096]{1,0:T(8,128)(2,1)} async-done(((bf16[320,4096]{1,0:T(8,128)(2,1)}), bf16[320,4096]{1,0:T(8,128)(2,1)}) %all-reduce.2.cloned.1.call-update) | async-done | bytes 2621456 | tf_op jit(solution)/shard_map/psum | solution.py:133
  268.1 0.7 collective-permute-start.1
  268.8 3.7 %fusion.12 = (bf16[10240,128]{1,0:T(8,128)(2,1)S(1)}, bf16[10240,128]{1,0:T(8,128)(2,1)}) fusion(bf16[10240,256]{1,0:T(8,128)(2,1)} %bitcast.38), kind=kLoop, calls=%fused_computation.55 | loop fusion | bytes 10485760 | tf_op jit(solution)/shard_map/slice | solution.py:185
  272.5 3.8 %gather_fusion = bf16[704,128]{1,0:T(8,128)(2,1)S(1)} fusion(bf16[10240,128]{1,0:T(8,128)(2,1)} %get-tuple-element.12, s32[1024]{0:T(1024)S(1)} %pad_clamp_fusion), kind=kCustom, calls=%fused_computation.clone | custom fusion | bytes 363264 | tf_op jit(solution)/shard_map/jit(_take)/gather | solution.py:189
  276.3 2.0 gather_fusion.1
  278.4 1.0 select_select_fusion
  279.4 0.0 collective-permute-done.1
  279.4 2.9 broadcast_select_fusion.1
  282.2 2.7 pad_maximum_fusion.2.projected_ref
  284.9 10.0 %shard_map.95 = bf16[320,8192]{1,0:T(8,128)(2,1)} custom-call(bf16[320,8192]{1,0:T(8,128)(2,1)} %pad_maximum_fusion.2.projected_ref, bf16[320,8192]{1,0:T(8,128)(2,1)} %residual_ref.1, bf16[1,8192]{1,0:T(2,128)(2,1)} %reshape.252.gain_ref), custom_call_target="tpu_custom_call" | custom-call | flops 13107200 | bytes 15728640 | tf_op jit(solution)/shard_map/pallas_call | solution.py:109
  (12 shorter events, 0.2 us)
Async XLA Ops:
  7.2 138.4 %all-gather.2.cloned.1.call-start = ((), (), s32[]{:S(2)}) async-start(), calls=%async_computation | async-start | bytes 14057472 | tf_op jit(solution)/shard_map/all_gather | solution.py:147
  9.0 259.1 %all-reduce.2.cloned.1.call-start = ((), (), s32[]{:S(2)}) async-start(), calls=%async_computation.1 | async-start | bytes 5242880 | tf_op jit(solution)/shard_map/psum | solution.py:133
  148.4 2.3 copy-start.1
  156.1 2.8 copy-start
  182.7 2.4 copy-start.2
  186.8 7.9 %collective-permute-start = (bf16[320,4096]{1,0:T(8,128)(2,1)}, bf16[320,4096]{1,0:T(8,128)(2,1)S(1)}, u32[]{:S(2)}, u32[]{:S(2)}) collective-permute-start(bf16[320,4096]{1,0:T(8,128)(2,1)} %constant_dynamic-slice_fusion), channel_id=1, source_target_pairs={{0,1},{1,0},{2,3},{3,2},{4,5},{5,4},{6,7},{7,6},{8,9},{9,8},{10,11... | collective-permute-start | bytes 7864328 | tf_op jit(solution)/shard_map/ppermute | solution.py:131
  190.0 9.0 %copy-start.3 = (bf16[8192]{0:T(1024)(128)(2,1)S(1)}, bf16[8192]{0:T(1024)(128)(2,1)}, u32[]{:S(2)}) copy-start(bf16[8192]{0:T(1024)(128)(2,1)} %param.14) | copy-start | bytes 49156
  190.0 9.6 %copy-start.4 = (s32[18]{0:T(128)S(1)}, s32[18]{0:T(128)}, u32[]{:S(2)}) copy-start(s32[18]{0:T(128)} %param.15) | copy-start | bytes 220
  268.1 11.3 %collective-permute-start.1 = (bf16[320,4096]{1,0:T(8,128)(2,1)}, bf16[320,4096]{1,0:T(8,128)(2,1)}, u32[]{:S(2)}, u32[]{:S(2)}) collective-permute-start(bf16[320,4096]{1,0:T(8,128)(2,1)} %all-reduce.2.cloned.1.call-done), channel_id=1, source_target_pairs={{0,1},{1,0},{2,3},{3,2},{4,5},{5,4},{6,7},{7,6},{8,9},{9,8},{10,11... | collective-permute-start | bytes 7864328 | tf_op jit(solution)/shard_map/ppermute | solution.py:134
Sparse Core Ops, SparseCore 0:
  11.0 134.4 all-gather.1
  199.1 68.9 all-reduce.1

commit v4 on v2

--- a/solution.py
+++ b/solution.py
@@ -56,14 +56,37 @@
     return (doc_start + within, is_live)
 
 
-def attn_kernel(q_ref, kv_ref, qpos_ref, qseg_ref, kpos_ref, kseg_ref, o_ref, *, heads, scale):
+def attn_kernel(
+    first_ref, q_ref, g_hbm, qpos_ref, qseg_ref, kpos_ref, kseg_ref, o_ref, window, sems,
+    *, heads, scale, blocks, half, seq_count, kv_cols,
+):
+    first = first_ref[pl.program_id(0)]
+    copies = []
+    for k in range(blocks):
+        block = first + k
+        upper = block >= seq_count
+        row = jnp.where(upper, half, 0)
+        device = jnp.where(upper, 2 * seq_count - 1 - block, block)
+        copy = pltpu.make_async_copy(
+            g_hbm.at[pl.ds(row, half), pl.ds(device * kv_cols, kv_cols)],
+            window.at[pl.ds(k * half, half)],
+            sems.at[k],
+        )
+        copy.start()
+        copies.append(copy)
+    pad = window.shape[0] - blocks * half
+    if pad:
+        window[pl.ds(blocks * half, pad), :] = jnp.zeros((pad, kv_cols), window.dtype)
+    for copy in copies:
+        copy.wait()
     allowed = (kpos_ref[0] <= qpos_ref[0]) & (kseg_ref[0] == qseg_ref[0])
-    key = kv_ref[0, :, :HD]
-    value = kv_ref[0, :, HD:]
+    key = window[:, :HD]
+    value = window[:, HD:]
     for h in range(heads):
         query = q_ref[0, :, h * HD:(h + 1) * HD]
-        scores = lax.dot_general(query, key, (((1,), (1,)), ((), ())),
-                                 preferred_element_type=jnp.float32) * scale
+        scores = lax.dot_general(
+            query, key, (((1,), (1,)), ((), ())), preferred_element_type=jnp.float32
+        ) * scale
         scores = jnp.where(allowed, scores, -1e30)
         top = jnp.max(scores, axis=1, keepdims=True)
         weights = jnp.where(allowed, jnp.exp(scores - top), 0.0)
@@ -71,29 +94,44 @@
         summed = jnp.dot(weights.astype(jnp.bfloat16), value, preferred_element_type=jnp.float32)
         o_ref[0, :, h * HD:(h + 1) * HD] = (summed / total).astype(o_ref.dtype)
 
-def attend(q, kv, qpos, qseg, kpos, kseg):
-    blocks, rows, width = q.shape
-    window = kv.shape[1]
+
+def attend(first, q, gathered, qpos, qseg, kpos, kseg, blocks, seq_count, kv_cols):
+    count, rows, width = q.shape
+    window_rows = kpos.shape[-1]
     heads = width // HD
-    kern = functools.partial(attn_kernel, heads=heads, scale=1.0 / math.sqrt(HD))
+    kern = functools.partial(
+        attn_kernel, heads=heads, scale=1.0 / math.sqrt(HD), blocks=blocks, half=rows,
+        seq_count=seq_count, kv_cols=kv_cols,
+    )
+    grid_spec = pltpu.PrefetchScalarGridSpec(
+        num_scalar_prefetch=1,
+        grid=(count,),
+        in_specs=[
+            pl.BlockSpec((1, rows, width), lambda b, f: (b, 0, 0)),
+            pl.BlockSpec(memory_space=pl.ANY),
+            pl.BlockSpec((1, rows, 1), lambda b, f: (b, 0, 0)),
+            pl.BlockSpec((1, rows, 1), lambda b, f: (b, 0, 0)),
+            pl.BlockSpec((1, 1, window_rows), lambda b, f: (b, 0, 0)),
+            pl.BlockSpec((1, 1, window_rows), lambda b, f: (b, 0, 0)),
+        ],
+        out_specs=pl.BlockSpec((1, rows, width), lambda b, f: (b, 0, 0)),
+        scratch_shapes=[
+            pltpu.VMEM((window_rows, kv_cols), gathered.dtype),
+            pltpu.SemaphoreType.DMA((blocks,)),
+        ],
+    )
     return pl.pallas_call(
         kern,
-        grid=(blocks,),
-        in_specs=[
-            pl.BlockSpec((1, rows, width), lambda b: (b, 0, 0)),
-            pl.BlockSpec((1, window, 2 * HD), lambda b: (b, 0, 0)),
-            pl.BlockSpec((1, rows, 1), lambda b: (b, 0, 0)),
-            pl.BlockSpec((1, rows, 1), lambda b: (b, 0, 0)),
-            pl.BlockSpec((1, 1, window), lambda b: (b, 0, 0)),
-            pl.BlockSpec((1, 1, window), lambda b: (b, 0, 0)),
-        ],
-        out_specs=pl.BlockSpec((1, rows, width), lambda b: (b, 0, 0)),
-        out_shape=jax.ShapeDtypeStruct((blocks, rows, width), jnp.bfloat16),
+        grid_spec=grid_spec,
+        out_shape=jax.ShapeDtypeStruct((count, rows, width), jnp.bfloat16),
         compiler_params=pltpu.CompilerParams(vmem_limit_bytes=48 * 1024 * 1024),
-        cost_estimate=pl.CostEstimate(flops=4 * blocks * heads * rows * window * HD,
-                                      transcendentals=blocks * heads * rows * window,
-                                      bytes_accessed=blocks * (window * 2 * HD * 2 + 2 * rows * width * 2)),
-    )(q, kv, qpos, qseg, kpos, kseg)
+        cost_estimate=pl.CostEstimate(
+            flops=4 * count * heads * rows * window_rows * HD,
+            transcendentals=count * heads * rows * window_rows,
+            bytes_accessed=count * (window_rows * kv_cols * 2 + 2 * rows * width * 2),
+        ),
+    )(first, q, gathered, qpos, qseg, kpos, kseg)
+
 
 def norm_kernel(projected_ref, residual_ref, gain_ref, out_ref):
     hidden = residual_ref[...].astype(jnp.float32) + projected_ref[...].astype(jnp.float32)
@@ -137,27 +175,28 @@
         stacked[:per_device].reshape(per_device, seq_count, 2 * kv_width), (1, 0, 2)
     )
     kv_piece = kv_stored.reshape(seq_count * per_device, 2 * kv_width)
-    halves = kv_stored.reshape(seq_count, 2, half, 2 * kv_width)
-    kv_pos = jnp.concatenate([halves[:, 0], halves[::-1, 1]], axis=0).reshape(
-        seq_count * per_device, 2 * kv_width
-    )
-    window = min(seq_count * per_device, -(-(MAX_PROMPT - 1 + half) // 128) * 128)
+    blocks = min(2 * seq_count, -(-(MAX_PROMPT - 1) // half) + 1)
+    window = -(-(blocks * half) // 128) * 128
     block_index = jnp.stack([seq_index, 2 * seq_count - 1 - seq_index])
-    starts = jnp.clip(block_index * half + half - window, 0, seq_count * per_device - window)
-    kv_win = jnp.stack(
-        [lax.dynamic_slice_in_dim(kv_pos, starts[i], window, axis=0) for i in range(2)]
-    )
-    key_position = starts[:, None] + jnp.arange(window, dtype=jnp.int32)[None, :]
+    first = jnp.clip(block_index - (blocks - 1), 0, 2 * seq_count - blocks).astype(jnp.int32)
+    offsets = jnp.arange(window, dtype=jnp.int32)[None, :]
+    key_position = jnp.where(
+        offsets < blocks * half, first[:, None] * half + offsets, 4 * seq_count * per_device
+    )
     query_position = block_index[:, None] * half + jnp.arange(half, dtype=jnp.int32)[None, :]
     key_segment = segment_of(key_position.reshape(-1), prompt_lengths).reshape(2, 1, window)
     query_segment = segment_of(query_position.reshape(-1), prompt_lengths).reshape(2, half, 1)
     attended = attend(
+        first,
         queries.reshape(2, half, queries.shape[1]),
-        kv_win,
+        stacked,
         query_position[:, :, None],
         query_segment,
         key_position[:, None, :],
         key_segment,
+        blocks,
+        seq_count,
+        2 * kv_width,
     ).reshape(per_device, -1)
     partial_value = jnp.dot(attended, weight_full, preferred_element_type=jnp.float32)
     projected = lax.psum(partial_value.astype(jnp.bfloat16), "tensor")

time: 283 us -> 282 us (level)
  waiting for transfers between devices: 195 us -> 200 us
  between operations: 17.9 us -> 14.2 us
  other arithmetic: 9.96 us -> 6.71 us
  Pallas kernels: 27.2 us -> 30.2 us
    transpose x0 -> x1, local copies, waits for them, and re-layouts: none -> 5.27 us  [body(): jnp.transpose(stacked[:per_device].reshape(per_device, seq_count, 2 * kv_...]
    all_gather x1, waiting for transfers between devices: 126 us -> 130 us  [body(): lax.all_gather(jnp.concatenate([kv_rows, out_weight], axis=0), 'seq', axi...]
    reshape x1 -> x0, local copies, waits for them, and re-layouts: 3.12 us -> none  [body(): stacked[:per_device].reshape(per_device, seq_count, 2 * kv_width)]
    pallas_call x1, Pallas kernels: 17.2 us -> 20.2 us  [attend(): pl.pallas_call(kern, grid_spec=grid_spec, out_shape=jax.ShapeDtypeStruct(...]
  transfers between devices with their start and end apart: 2 -> 2, of which waited for: 2 -> 2; matrix products, arithmetic and copies ran while one was open for 7% -> 6% of each run, Pallas kernels for 0% -> 0%
where the time goes in v4:
time: 282 us; the launch traced here: 281 us
  waiting for transfers between devices  200 us (71%)
  Pallas kernels  30.2 us (11%)
  local copies, waits for them, and re-layouts  21.7 us (8%)
  between operations  14.2 us (5%)
  matrix products  8.63 us (3%)
  other arithmetic  6.71 us (2%)
    all_gather x1, waiting for transfers between devices, body(): lax.all_gather(jnp.concatenate([kv_rows, out_weight], axis=0), 'seq', axi...  130 us
    psum x1, waiting for transfers between devices, body(): projected = lax.psum(partial_value.astype(jnp.bfloat16), 'tensor')  70.1 us
    pallas_call x1, Pallas kernels, attend(): pl.pallas_call(kern, grid_spec=grid_spec, out_shape=jax.ShapeDtypeStruct(...  20.2 us
    pallas_call x1, Pallas kernels, residual_norm(): pl.pallas_call(norm_kernel, grid=(steps,), in_specs=[pl.BlockSpec((rows_p...  9.99 us
    dot_general x1, matrix products, body(): jnp.dot(attended, weight_full, preferred_element_type=jnp.float32)  8.63 us
  transfers between devices with their start and end apart: 2, of which 2 were waited for; matrix products, arithmetic and copies ran while one was open for 6% of the time, Pallas kernels for 0%

profile of v4, /device:TPU:1, one launch (start us, length us, event | category | flops | bytes accessed | tf_op | source)
XLA Modules:
  0.0 281.4 jit_solution(3656113116707772538)
XLA Ops:
  7.2 0.0 all-gather.2.cloned.1.call-start
  7.2 1.8 pad_maximum_fusion
  9.0 0.0 all-gather.2.cloned.1.call-update
  9.0 0.0 all-reduce.2.cloned.1.call-start
  9.1 0.7 fusion.15
  9.8 0.1 copy.19
  9.9 0.1 reduce.1
  10.0 0.1 broadcast_multiply_fusion
  10.1 0.1 add_select_fusion
  10.2 0.7 copy.17
  11.0 0.1 reduce
  11.1 0.3 convert_reduce_fusion
  11.5 0.1 iota_add_fusion.2
  11.5 0.1 add.137
  11.6 0.1 convert_reduce_fusion.1
  11.7 0.2 reshape.311.qseg_ref
  11.9 1.3 reshape.284.gain_ref
  13.3 0.7 fusion.10
  13.9 0.7 fusion.14
  14.6 0.8 fusion.4
  15.4 0.1 iota_add_fusion.qpos_ref
  15.5 0.1 broadcast_select_fusion.kpos_ref
  15.6 129.9 %all-gather.2.cloned.1.call-done.g_hbm = bf16[832,8192]{1,0:T(8,128)(2,1)} async-done(((bf16[832,256]{1,0:T(8,128)(2,1)}), bf16[832,8192]{1,0:T(8,128)(2,1)}) %all-gather.2.cloned.1.call-update) | async-done | bytes 13631504 | tf_op jit(solution)/shard_map/all_gather | solution.py:170
  145.5 0.0 slice-start
  145.5 2.5 slice-done
  148.0 1.8 copy.21
  149.8 0.0 copy-start
  149.8 5.3 %copy.20 = bf16[32,320,256]{2,1,0:T(8,128)(2,1)} copy(bf16[32,320,256]{2,0,1:T(8,128)(2,1)S(1)} %bitcast.17) | data formatting | bytes 10485760 | tf_op jit(solution)/shard_map/transpose | solution.py:174
  155.1 0.0 copy-done
  155.1 20.2 %shard_map.94 = bf16[2,160,512]{2,1,0:T(8,128)(2,1)S(1)} custom-call(s32[2]{0:T(128)S(1)} %get-tuple-element.10.first_ref, bf16[2,160,512]{2,1,0:T(8,128)(2,1)S(1)} %bitcast.13, bf16[832,8192]{1,0:T(8,128)(2,1)} %all-gather.2.cloned.1.call-done.g_hbm, s32[2,160,1]{2,1,0:T(8,128)S(1)} %iota_add_fusion.qpos_ref, s32[2,160,1]{2,1,0:T(8,128)S(1)} %reshape.311.qseg_ref, ...), custom_call_target="tpu_custom_call" | custom-call | flops 3523215360 | bytes 6160384 | tf_op jit(solution)/shard_map/pallas_call | solution.py:123
  175.2 8.6 %convolution_convert_fusion = bf16[320,8192]{1,0:T(8,128)(2,1)} fusion(bf16[320,512]{1,0:T(8,128)(2,1)S(1)} %bitcast.14, bf16[832,8192]{1,0:T(8,128)(2,1)} %all-gather.2.cloned.1.call-done.g_hbm), kind=kOutput, calls=%fused_computation.2 | convolution fusion | flops 2686976000 | bytes 13959168 | tf_op jit(solution)/shard_map/dot_general | solution.py:201
  183.9 0.0 all-reduce.2.cloned.1.call-update
  183.9 3.7 %fusion.12 = (bf16[10240,128]{1,0:T(8,128)(2,1)S(1)}, bf16[10240,128]{1,0:T(8,128)(2,1)}) fusion(bf16[10240,256]{1,0:T(8,128)(2,1)} %bitcast.16), kind=kLoop, calls=%fused_computation.46 | loop fusion | bytes 10485760 | tf_op jit(solution)/shard_map/slice | solution.py:209
  187.6 3.8 %gather_fusion = bf16[704,128]{1,0:T(8,128)(2,1)S(1)} fusion(bf16[10240,128]{1,0:T(8,128)(2,1)} %get-tuple-element.12, s32[1024]{0:T(1024)S(1)} %pad_clamp_fusion), kind=kCustom, calls=%fused_computation.clone | custom fusion | bytes 363264 | tf_op jit(solution)/shard_map/jit(_take)/gather | solution.py:213
  191.5 2.0 gather_fusion.1
  193.5 1.0 select_select_fusion
  194.5 70.1 %all-reduce.2.cloned.1.call-done.projected_ref = bf16[320,8192]{1,0:T(8,128)(2,1)} async-done(((bf16[320,8192]{1,0:T(8,128)(2,1)}), bf16[320,8192]{1,0:T(8,128)(2,1)}) %all-reduce.2.cloned.1.call-update) | async-done | bytes 5242896 | tf_op jit(solution)/shard_map/psum | solution.py:202
  264.6 10.0 %shard_map.95 = bf16[320,8192]{1,0:T(8,128)(2,1)} custom-call(bf16[320,8192]{1,0:T(8,128)(2,1)} %all-reduce.2.cloned.1.call-done.projected_ref, bf16[320,8192]{1,0:T(8,128)(2,1)} %residual_ref.1, bf16[1,8192]{1,0:T(2,128)(2,1)} %reshape.284.gain_ref), custom_call_target="tpu_custom_call" | custom-call | flops 13107200 | bytes 15728640 | tf_op jit(solution)/shard_map/pallas_call | solution.py:147
  (10 shorter events, 0.2 us)
Async XLA Ops:
  7.2 138.4 %all-gather.2.cloned.1.call-start = ((), (), s32[]{:S(2)}) async-start(), calls=%async_computation | async-start | bytes 14057472 | tf_op jit(solution)/shard_map/all_gather | solution.py:170
  9.0 255.6 %all-reduce.2.cloned.1.call-start = ((), (), s32[]{:S(2)}) async-start(), calls=%async_computation.1 | async-start | bytes 10485760 | tf_op jit(solution)/shard_map/psum | solution.py:202
  145.5 2.5 slice-start
  149.8 5.3 %copy-start = (bf16[320,512]{1,0:T(8,128)(2,1)S(1)}, bf16[320,512]{1,0:T(8,128)(2,1)}, u32[]{:S(2)}) copy-start(bf16[320,512]{1,0:T(8,128)(2,1)} %param.9) | copy-start | bytes 983044
Sparse Core Ops, SparseCore 0:
  11.0 134.4 all-gather.1
  184.0 80.5 all-reduce.1

commit v5 on v4

--- a/solution.py
+++ b/solution.py
@@ -171,10 +171,6 @@
         jnp.concatenate([kv_rows, out_weight], axis=0), "seq", axis=1, tiled=True
     )
     weight_full = stacked[per_device:]
-    kv_stored = jnp.transpose(
-        stacked[:per_device].reshape(per_device, seq_count, 2 * kv_width), (1, 0, 2)
-    )
-    kv_piece = kv_stored.reshape(seq_count * per_device, 2 * kv_width)
     blocks = min(2 * seq_count, -(-(MAX_PROMPT - 1) // half) + 1)
     window = -(-(blocks * half) // 128) * 128
     block_index = jnp.stack([seq_index, 2 * seq_count - 1 - seq_index])
@@ -199,19 +195,20 @@
         2 * kv_width,
     ).reshape(per_device, -1)
     partial_value = jnp.dot(attended, weight_full, preferred_element_type=jnp.float32)
-    projected = lax.psum(partial_value.astype(jnp.bfloat16), "tensor")
+    partial_value, stacked = lax.optimization_barrier((partial_value.astype(jnp.bfloat16), stacked))
+    projected = lax.psum(partial_value, "tensor")
     normed = residual_norm(projected, residual_in, norm_gain)
     slot_ids = seq_index * SLOT_DEV + jnp.arange(SLOT_DEV, dtype=jnp.int32)
     source, is_live = slot_source(slot_ids, prompt_lengths, PAGE)
     target = stored_row(source, per_device, seq_count)
     empty_cache = jnp.zeros((SLOT_DEV, kv_width), jnp.bfloat16)
-    key_piece = kv_piece[:, :kv_width]
-    value_piece = kv_piece[:, kv_width:]
-    piece_rows = key_piece.shape[0]
+    kv_grid = stacked[:per_device].reshape(per_device, seq_count, 2 * kv_width)
+    piece_rows = seq_count * per_device
     found = is_live & (target >= 0) & (target < piece_rows)
     safe_index = jnp.clip(target, 0, piece_rows - 1)
-    cache_keys = jnp.where(found[:, None], jnp.take(key_piece, safe_index, axis=0), empty_cache)
-    cache_values = jnp.where(found[:, None], jnp.take(value_piece, safe_index, axis=0), empty_cache)
+    cache_rows = kv_grid[safe_index % per_device, safe_index // per_device]
+    cache_keys = jnp.where(found[:, None], cache_rows[:, :kv_width], empty_cache)
+    cache_values = jnp.where(found[:, None], cache_rows[:, kv_width:], empty_cache)
     return (normed, cache_keys, cache_values)
 
 

time: 282 us -> 274 us (0.972)
  waiting for transfers between devices: 200 us -> 194 us
    psum x1, waiting for transfers between devices: 70.1 us -> 59.6 us  [body(): projected = lax.psum(partial_value, 'tensor')]
    gather x2 -> x1, local copies, waits for them, and re-layouts: 5.84 us -> 11.8 us  [body(): cache_rows = kv_grid[safe_index % per_device, safe_index // per_device]]
    transpose x1 -> x0, local copies, waits for them, and re-layouts: 5.27 us -> none  [body(): jnp.transpose(stacked[:per_device].reshape(per_device, seq_count, 2 * kv_...]
    all_gather x1, waiting for transfers between devices: 130 us -> 134 us  [body(): lax.all_gather(jnp.concatenate([kv_rows, out_weight], axis=0), 'seq', axi...]
    unnamed x3 -> x7, local copies, waits for them, and re-layouts: 1.77 us -> 5.69 us
    slice x3 -> x2, local copies, waits for them, and re-layouts: 6.23 us -> 2.48 us  [body(): kv_grid = stacked[:per_device].reshape(per_device, seq_count, 2 * kv_width)]
  transfers between devices with their start and end apart: 2 -> 2, of which waited for: 2 -> 2; matrix products, arithmetic and copies ran while one was open for 6% -> 7% of each run, Pallas kernels for 0% -> 0%
where the time goes in v5:
time: 274 us; the launch traced here: 273 us
  waiting for transfers between devices  194 us (71%)
  Pallas kernels  30.2 us (11%)
  local copies, waits for them, and re-layouts  21.8 us (8%)
  between operations  14.1 us (5%)
  matrix products  8.63 us (3%)
  other arithmetic  4.07 us (1%)
    all_gather x1, waiting for transfers between devices, body(): lax.all_gather(jnp.concatenate([kv_rows, out_weight], axis=0), 'seq', axi...  134 us
    psum x1, waiting for transfers between devices, body(): projected = lax.psum(partial_value, 'tensor')  59.6 us
    pallas_call x1, Pallas kernels, attend(): pl.pallas_call(kern, grid_spec=grid_spec, out_shape=jax.ShapeDtypeStruct(...  20.2 us
    gather x1, local copies, waits for them, and re-layouts, body(): cache_rows = kv_grid[safe_index % per_device, safe_index // per_device]  11.8 us
    pallas_call x1, Pallas kernels, residual_norm(): pl.pallas_call(norm_kernel, grid=(steps,), in_specs=[pl.BlockSpec((rows_p...  9.99 us
    dot_general x1, matrix products, body(): jnp.dot(attended, weight_full, preferred_element_type=jnp.float32)  8.63 us
    unnamed x7, local copies, waits for them, and re-layouts  5.69 us
  transfers between devices with their start and end apart: 2, of which 2 were waited for; matrix products, arithmetic and copies ran while one was open for 7% of the time, Pallas kernels for 0%

profile of v5, /device:TPU:1, one launch (start us, length us, event | category | flops | bytes accessed | tf_op | source)
XLA Modules:
  0.0 272.9 jit_solution(8809437418868330451)
XLA Ops:
  7.2 0.0 all-gather.2.cloned.1.call-start
  7.2 1.8 pad_maximum_fusion
  9.0 0.0 all-gather.2.cloned.1.call-update
  9.0 0.0 all-reduce.2.cloned.1.call-start
  9.1 0.1 broadcast_multiply_fusion
  9.2 0.1 add_select_fusion
  9.3 0.7 copy.15
  10.1 0.1 reduce
  10.2 0.3 convert_reduce_fusion
  10.5 0.1 iota_add_fusion.2
  10.6 0.1 add.242
  10.7 0.1 convert_reduce_fusion.1
  10.8 0.2 reshape.407.qseg_ref
  11.0 0.1 iota_add_fusion.qpos_ref
  11.1 0.1 broadcast_select_fusion.kpos_ref
  11.2 134.3 %all-gather.2.cloned.1.call-done.g_hbm = bf16[832,8192]{1,0:T(8,128)(2,1)} async-done(((bf16[832,256]{1,0:T(8,128)(2,1)}), bf16[832,8192]{1,0:T(8,128)(2,1)}) %all-gather.2.cloned.1.call-update) | async-done | bytes 13631504 | tf_op jit(solution)/shard_map/all_gather | solution.py:170
  145.5 0.0 copy-start
  145.5 1.0 copy-done
  146.5 20.2 %shard_map.94 = bf16[2,160,512]{2,1,0:T(8,128)(2,1)S(1)} custom-call(s32[2]{0:T(128)S(1)} %get-tuple-element.11.first_ref, bf16[2,160,512]{2,1,0:T(8,128)(2,1)S(1)} %bitcast.10, bf16[832,8192]{1,0:T(8,128)(2,1)} %all-gather.2.cloned.1.call-done.g_hbm, s32[2,160,1]{2,1,0:T(8,128)S(1)} %iota_add_fusion.qpos_ref, s32[2,160,1]{2,1,0:T(8,128)S(1)} %reshape.407.qseg_ref, ...), custom_call_target="tpu_custom_call" | custom-call | flops 3523215360 | bytes 6160384 | tf_op jit(solution)/shard_map/pallas_call | solution.py:123
  166.7 8.6 %convolution_convert_fusion = bf16[320,8192]{1,0:T(8,128)(2,1)} fusion(bf16[320,512]{1,0:T(8,128)(2,1)S(1)} %bitcast.11, bf16[832,8192]{1,0:T(8,128)(2,1)} %all-gather.2.cloned.1.call-done.g_hbm), kind=kOutput, calls=%fused_computation.1 | convolution fusion | flops 2686976000 | bytes 13959168 | tf_op jit(solution)/shard_map/dot_general | solution.py:197
  175.3 0.0 copy-start.2
  175.3 0.0 copy-start.1
  175.3 0.0 all-reduce.2.cloned.1.call-update
  175.3 0.6 copy-done.2
  176.0 0.1 copy.17
  176.1 0.1 reduce.1
  176.2 0.0 copy-done.1
  176.2 0.6 reshape.397.gain_ref
  176.9 0.1 fusion.4
  177.0 0.1 fusion.18
  177.1 0.0 slice-start
  177.2 2.5 slice-done
  179.6 4.1 %copy.18 = bf16[40,8,32,256]{3,2,1,0:T(8,128)(2,1)} copy(bf16[40,8,32,256]{3,1,2,0:T(8,128)(2,1)S(1)} %bitcast.12) | data formatting | bytes 10485760
  183.7 11.8 %gather_fusion = bf16[704,256]{1,0:T(8,128)(2,1)S(1)} fusion(bf16[320,32,256]{2,1,0:T(8,128)(2,1)} %bitcast.13, s32[704]{0:T(1024)S(1)} %fusion.18), kind=kCustom, calls=%fused_computation | custom fusion | bytes 726528 | tf_op jit(solution)/shard_map/gather | solution.py:209
  195.5 0.9 slice_select_fusion
  196.4 59.6 %all-reduce.2.cloned.1.call-done.projected_ref = bf16[320,8192]{1,0:T(8,128)(2,1)} async-done(((bf16[320,8192]{1,0:T(8,128)(2,1)}), bf16[320,8192]{1,0:T(8,128)(2,1)}) %all-reduce.2.cloned.1.call-update) | async-done | bytes 5242896 | tf_op jit(solution)/shard_map/psum | solution.py:199
  256.1 10.0 %shard_map.95 = bf16[320,8192]{1,0:T(8,128)(2,1)} custom-call(bf16[320,8192]{1,0:T(8,128)(2,1)} %all-reduce.2.cloned.1.call-done.projected_ref, bf16[320,8192]{1,0:T(8,128)(2,1)} %residual_ref.1, bf16[1,8192]{1,0:T(2,128)(2,1)} %reshape.397.gain_ref), custom_call_target="tpu_custom_call" | custom-call | flops 13107200 | bytes 15728640 | tf_op jit(solution)/shard_map/pallas_call | solution.py:147
  (10 shorter events, 0.2 us)
Async XLA Ops:
  7.2 138.4 %all-gather.2.cloned.1.call-start = ((), (), s32[]{:S(2)}) async-start(), calls=%async_computation | async-start | bytes 14057472 | tf_op jit(solution)/shard_map/all_gather | solution.py:170
  9.0 247.0 %all-reduce.2.cloned.1.call-start = ((), (), s32[]{:S(2)}) async-start(), calls=%async_computation.1 | async-start | bytes 10485760 | tf_op jit(solution)/shard_map/psum | solution.py:199
  145.5 1.0 copy-start
  175.3 0.7 copy-start.2
  175.3 0.9 copy-start.1
  177.1 2.5 slice-start
Sparse Core Ops, SparseCore 0:
  11.0 134.4 all-gather.1
  175.5 80.5 all-reduce.1

commit v6 on v5

--- a/solution.py
+++ b/solution.py
@@ -58,9 +58,18 @@
 
 def attn_kernel(
     first_ref, q_ref, g_hbm, qpos_ref, qseg_ref, kpos_ref, kseg_ref, o_ref, window, sems,
-    *, heads, scale, blocks, half, seq_count, kv_cols,
+    weight, weight_sem, attended, *, heads, scale, blocks, half, seq_count, kv_cols, weight_row,
 ):
-    first = first_ref[pl.program_id(0)]
+    step = pl.program_id(0)
+    first = first_ref[step]
+    weight_copy = pltpu.make_async_copy(
+        g_hbm.at[pl.ds(weight_row, weight.shape[0])], weight, weight_sem.at[0]
+    )
+
+    @pl.when(step == 0)
+    def _():
+        weight_copy.start()
+
     copies = []
     for k in range(blocks):
         block = first + k
@@ -92,16 +101,29 @@
         weights = jnp.where(allowed, jnp.exp(scores - top), 0.0)
         total = jnp.sum(weights, axis=1, keepdims=True)
         summed = jnp.dot(weights.astype(jnp.bfloat16), value, preferred_element_type=jnp.float32)
-        o_ref[0, :, h * HD:(h + 1) * HD] = (summed / total).astype(o_ref.dtype)
+        attended[:, h * HD:(h + 1) * HD] = (summed / total).astype(attended.dtype)
+
+    @pl.when(step == 0)
+    def _():
+        weight_copy.wait()
+
+    out_cols = o_ref.shape[2]
+    chunk = 1024 if out_cols % 1024 == 0 else out_cols
+    for c in range(out_cols // chunk):
+        o_ref[0, :, c * chunk:(c + 1) * chunk] = jnp.dot(
+            attended[...], weight[:, c * chunk:(c + 1) * chunk], preferred_element_type=jnp.float32
+        ).astype(o_ref.dtype)
 
 
 def attend(first, q, gathered, qpos, qseg, kpos, kseg, blocks, seq_count, kv_cols):
     count, rows, width = q.shape
     window_rows = kpos.shape[-1]
     heads = width // HD
+    weight_row = count * rows
+    out_cols = gathered.shape[1]
     kern = functools.partial(
         attn_kernel, heads=heads, scale=1.0 / math.sqrt(HD), blocks=blocks, half=rows,
-        seq_count=seq_count, kv_cols=kv_cols,
+        seq_count=seq_count, kv_cols=kv_cols, weight_row=weight_row,
     )
     grid_spec = pltpu.PrefetchScalarGridSpec(
         num_scalar_prefetch=1,
@@ -114,21 +136,25 @@
             pl.BlockSpec((1, 1, window_rows), lambda b, f: (b, 0, 0)),
             pl.BlockSpec((1, 1, window_rows), lambda b, f: (b, 0, 0)),
         ],
-        out_specs=pl.BlockSpec((1, rows, width), lambda b, f: (b, 0, 0)),
+        out_specs=pl.BlockSpec((1, rows, out_cols), lambda b, f: (b, 0, 0)),
         scratch_shapes=[
             pltpu.VMEM((window_rows, kv_cols), gathered.dtype),
             pltpu.SemaphoreType.DMA((blocks,)),
+            pltpu.VMEM((gathered.shape[0] - weight_row, out_cols), gathered.dtype),
+            pltpu.SemaphoreType.DMA((1,)),
+            pltpu.VMEM((rows, width), jnp.bfloat16),
         ],
     )
     return pl.pallas_call(
         kern,
         grid_spec=grid_spec,
-        out_shape=jax.ShapeDtypeStruct((count, rows, width), jnp.bfloat16),
-        compiler_params=pltpu.CompilerParams(vmem_limit_bytes=48 * 1024 * 1024),
+        out_shape=jax.ShapeDtypeStruct((count, rows, out_cols), jnp.bfloat16),
+        compiler_params=pltpu.CompilerParams(vmem_limit_bytes=56 * 1024 * 1024),
         cost_estimate=pl.CostEstimate(
-            flops=4 * count * heads * rows * window_rows * HD,
+            flops=4 * count * heads * rows * window_rows * HD + 2 * count * rows * width * out_cols,
             transcendentals=count * heads * rows * window_rows,
-            bytes_accessed=count * (window_rows * kv_cols * 2 + 2 * rows * width * 2),
+            bytes_accessed=count * (window_rows * kv_cols * 2 + rows * width * 2 + rows * out_cols * 2)
+            + (gathered.shape[0] - weight_row) * out_cols * 2,
         ),
     )(first, q, gathered, qpos, qseg, kpos, kseg)
 
@@ -170,7 +196,6 @@
     stacked = lax.all_gather(
         jnp.concatenate([kv_rows, out_weight], axis=0), "seq", axis=1, tiled=True
     )
-    weight_full = stacked[per_device:]
     blocks = min(2 * seq_count, -(-(MAX_PROMPT - 1) // half) + 1)
     window = -(-(blocks * half) // 128) * 128
     block_index = jnp.stack([seq_index, 2 * seq_count - 1 - seq_index])
@@ -182,7 +207,7 @@
     query_position = block_index[:, None] * half + jnp.arange(half, dtype=jnp.int32)[None, :]
     key_segment = segment_of(key_position.reshape(-1), prompt_lengths).reshape(2, 1, window)
     query_segment = segment_of(query_position.reshape(-1), prompt_lengths).reshape(2, half, 1)
-    attended = attend(
+    partial_value = attend(
         first,
         queries.reshape(2, half, queries.shape[1]),
         stacked,
@@ -194,8 +219,7 @@
         seq_count,
         2 * kv_width,
     ).reshape(per_device, -1)
-    partial_value = jnp.dot(attended, weight_full, preferred_element_type=jnp.float32)
-    partial_value, stacked = lax.optimization_barrier((partial_value.astype(jnp.bfloat16), stacked))
+    partial_value, stacked = lax.optimization_barrier((partial_value, stacked))
     projected = lax.psum(partial_value, "tensor")
     normed = residual_norm(projected, residual_in, norm_gain)
     slot_ids = seq_index * SLOT_DEV + jnp.arange(SLOT_DEV, dtype=jnp.int32)

time: 274 us -> 270 us (0.985)
  matrix products: 8.63 us -> 0 us
  Pallas kernels: 30.2 us -> 36.5 us
  waiting for transfers between devices: 194 us -> 191 us
    dot_general x1 -> x0, matrix products: 8.63 us -> none  [body(): jnp.dot(attended, weight_full, preferred_element_type=jnp.float32)]
    pallas_call x1, Pallas kernels: 20.2 us -> 26.5 us  [attend(): pl.pallas_call(kern, grid_spec=grid_spec, out_shape=jax.ShapeDtypeStruct(...]
    all_gather x1, waiting for transfers between devices: 134 us -> 131 us  [body(): lax.all_gather(jnp.concatenate([kv_rows, out_weight], axis=0), 'seq', axi...]
    unnamed x7 -> x5, local copies, waits for them, and re-layouts: 5.69 us -> 4.7 us
  transfers between devices with their start and end apart: 2 -> 2, of which waited for: 2 -> 2; matrix products, arithmetic and copies ran while one was open for 7% -> 9% of each run, Pallas kernels for 0% -> 0%
where the time goes in v6:
time: 270 us
  waiting for transfers between devices  191 us (71%)
  Pallas kernels  36.5 us (14%)
  local copies, waits for them, and re-layouts  22.2 us (8%)
  between operations  14.1 us (5%)
  other arithmetic  5.91 us (2%)
    all_gather x1, waiting for transfers between devices, body(): lax.all_gather(jnp.concatenate([kv_rows, out_weight], axis=0), 'seq', axi...  131 us
    psum x1, waiting for transfers between devices, body(): projected = lax.psum(partial_value, 'tensor')  59.6 us
    pallas_call x1, Pallas kernels, attend(): pl.pallas_call(kern, grid_spec=grid_spec, out_shape=jax.ShapeDtypeStruct(...  26.5 us
    gather x1, local copies, waits for them, and re-layouts, body(): cache_rows = kv_grid[safe_index % per_device, safe_index // per_device]  11.8 us
    pallas_call x1, Pallas kernels, residual_norm(): pl.pallas_call(norm_kernel, grid=(steps,), in_specs=[pl.BlockSpec((rows_p...  9.99 us
  transfers between devices with their start and end apart: 2, of which 2 were waited for; matrix products, arithmetic and copies ran while one was open for 9% of the time, Pallas kernels for 0%

profile of v6, /device:TPU:1, one launch (start us, length us, event | category | flops | bytes accessed | tf_op | source)
XLA Modules:
  0.0 269.7 jit_solution(4814700785315469942)
XLA Ops:
  7.2 0.0 all-gather.2.cloned.1.call-start
  7.2 1.8 pad_maximum_fusion
  9.0 0.0 all-gather.2.cloned.1.call-update
  9.0 0.0 all-reduce.2.cloned.1.call-start
  9.1 0.7 broadcast_multiply_fusion
  9.8 0.1 add_select_fusion
  9.9 0.7 copy.15
  10.7 0.1 reduce
  10.8 0.3 convert_reduce_fusion
  11.1 0.7 reshape.395.kseg_ref
  11.7 0.1 iota_add_fusion.2
  11.8 0.1 add.242
  11.9 0.1 convert_reduce_fusion.1
  12.0 0.9 reshape.407.qseg_ref
  12.9 0.7 iota_add_fusion.qpos_ref
  13.6 0.7 broadcast_select_fusion.kpos_ref
  14.3 131.2 %all-gather.2.cloned.1.call-done.g_hbm = bf16[832,8192]{1,0:T(8,128)(2,1)} async-done(((bf16[832,256]{1,0:T(8,128)(2,1)}), bf16[832,8192]{1,0:T(8,128)(2,1)}) %all-gather.2.cloned.1.call-update) | async-done | bytes 13631504 | tf_op jit(solution)/shard_map/all_gather | solution.py:196
  145.5 26.5 %shard_map.94 = bf16[2,160,8192]{2,1,0:T(8,128)(2,1)} custom-call(s32[2]{0:T(128)} %get-tuple-element.11.first_ref, bf16[2,160,512]{2,1,0:T(8,128)(2,1)} %bitcast.13, bf16[832,8192]{1,0:T(8,128)(2,1)} %all-gather.2.cloned.1.call-done.g_hbm, s32[2,160,1]{2,1,0:T(8,128)} %iota_add_fusion.qpos_ref, s32[2,160,1]{2,1,0:T(8,128)} %reshape.407.qseg_ref, ...), custom_call_target="tpu_custom_call" | custom-call | flops 6207569920 | bytes 19464192 | tf_op jit(solution)/shard_map/pallas_call | solution.py:148
  172.1 0.0 copy-start.1
  172.1 0.0 copy-start
  172.1 0.0 all-reduce.2.cloned.1.call-update
  172.1 0.6 copy-done.1
  172.8 0.1 copy.17
  172.9 0.1 reduce.1
  173.0 0.0 copy-done
  173.0 0.6 reshape.397.gain_ref
  173.7 0.1 fusion.3
  173.8 0.1 fusion.17
  173.9 0.0 slice-start
  173.9 2.5 slice-done
  176.4 4.1 %copy.18 = bf16[40,8,32,256]{3,2,1,0:T(8,128)(2,1)} copy(bf16[40,8,32,256]{3,1,2,0:T(8,128)(2,1)S(1)} %bitcast.9) | data formatting | bytes 10485760
  180.5 11.8 %gather_fusion = bf16[704,256]{1,0:T(8,128)(2,1)S(1)} fusion(bf16[320,32,256]{2,1,0:T(8,128)(2,1)} %bitcast.10, s32[704]{0:T(1024)S(1)} %fusion.17), kind=kCustom, calls=%fused_computation | custom fusion | bytes 726528 | tf_op jit(solution)/shard_map/gather | solution.py:233
  192.4 0.9 slice_select_fusion
  193.2 59.6 %all-reduce.2.cloned.1.call-done.projected_ref = bf16[320,8192]{1,0:T(8,128)(2,1)} async-done(((bf16[320,8192]{1,0:T(8,128)(2,1)}), bf16[320,8192]{1,0:T(8,128)(2,1)}) %all-reduce.2.cloned.1.call-update) | async-done | bytes 5242896 | tf_op jit(solution)/shard_map/psum | solution.py:223
  252.9 10.0 %shard_map.95 = bf16[320,8192]{1,0:T(8,128)(2,1)} custom-call(bf16[320,8192]{1,0:T(8,128)(2,1)} %all-reduce.2.cloned.1.call-done.projected_ref, bf16[320,8192]{1,0:T(8,128)(2,1)} %residual_ref.1, bf16[1,8192]{1,0:T(2,128)(2,1)} %reshape.397.gain_ref), custom_call_target="tpu_custom_call" | custom-call | flops 13107200 | bytes 15728640 | tf_op jit(solution)/shard_map/pallas_call | solution.py:173
  (9 shorter events, 0.2 us)
Async XLA Ops:
  7.2 138.4 %all-gather.2.cloned.1.call-start = ((), (), s32[]{:S(2)}) async-start(), calls=%async_computation | async-start | bytes 14057472 | tf_op jit(solution)/shard_map/all_gather | solution.py:196
  9.0 243.8 %all-reduce.2.cloned.1.call-start = ((), (), s32[]{:S(2)}) async-start(), calls=%async_computation.1 | async-start | bytes 10485760 | tf_op jit(solution)/shard_map/psum | solution.py:223
  172.1 0.7 copy-start.1
  172.1 0.9 copy-start
  173.9 2.5 slice-start
Sparse Core Ops, SparseCore 0:
  11.0 134.4 all-gather.1
  172.3 80.5 all-reduce.1

commit v7 on v6

--- a/solution.py
+++ b/solution.py
@@ -167,7 +167,7 @@
     ).astype(out_ref.dtype)
 
 
-def residual_norm(projected, residual, gain, rows_per_step=40):
+def residual_norm(projected, residual, gain, rows_per_step=80):
     rows, width = projected.shape
     steps = rows // rows_per_step
     return pl.pallas_call(

time: 270 us -> 269 us (level)
  no operation moved by 1% of the time
where the time goes in v7:
time: 269 us; the launch traced here: 268 us
  waiting for transfers between devices  191 us (71%)
  Pallas kernels  35 us (13%)
  local copies, waits for them, and re-layouts  22.1 us (8%)
  between operations  14.1 us (5%)
  other arithmetic  5.91 us (2%)
    all_gather x1, waiting for transfers between devices, body(): lax.all_gather(jnp.concatenate([kv_rows, out_weight], axis=0), 'seq', axi...  131 us
    psum x1, waiting for transfers between devices, body(): projected = lax.psum(partial_value, 'tensor')  59.6 us
    pallas_call x1, Pallas kernels, attend(): pl.pallas_call(kern, grid_spec=grid_spec, out_shape=jax.ShapeDtypeStruct(...  26.5 us
    gather x1, local copies, waits for them, and re-layouts, body(): cache_rows = kv_grid[safe_index % per_device, safe_index // per_device]  11.8 us
    pallas_call x1, Pallas kernels, residual_norm(): pl.pallas_call(norm_kernel, grid=(steps,), in_specs=[pl.BlockSpec((rows_p...  8.42 us
  transfers between devices with their start and end apart: 2, of which 2 were waited for; matrix products, arithmetic and copies ran while one was open for 9% of the time, Pallas kernels for 0%

profile of v7, /device:TPU:1, one launch (start us, length us, event | category | flops | bytes accessed | tf_op | source)
XLA Modules:
  0.0 268.1 jit_solution(13555326476647132213)
XLA Ops:
  7.2 0.0 all-gather.2.cloned.1.call-start
  7.2 1.8 pad_maximum_fusion
  9.0 0.0 all-gather.2.cloned.1.call-update
  9.0 0.0 all-reduce.2.cloned.1.call-start
  9.1 0.7 broadcast_multiply_fusion
  9.8 0.1 add_select_fusion
  9.9 0.7 copy.15
  10.7 0.1 reduce
  10.8 0.3 convert_reduce_fusion
  11.1 0.7 reshape.395.kseg_ref
  11.7 0.1 iota_add_fusion.2
  11.8 0.1 add.242
  11.9 0.1 convert_reduce_fusion.1
  12.0 0.9 reshape.407.qseg_ref
  12.9 0.7 iota_add_fusion.qpos_ref
  13.6 0.7 broadcast_select_fusion.kpos_ref
  14.3 131.2 %all-gather.2.cloned.1.call-done.g_hbm = bf16[832,8192]{1,0:T(8,128)(2,1)} async-done(((bf16[832,256]{1,0:T(8,128)(2,1)}), bf16[832,8192]{1,0:T(8,128)(2,1)}) %all-gather.2.cloned.1.call-update) | async-done | bytes 13631504 | tf_op jit(solution)/shard_map/all_gather | solution.py:196
  145.5 26.5 %shard_map.94 = bf16[2,160,8192]{2,1,0:T(8,128)(2,1)} custom-call(s32[2]{0:T(128)} %get-tuple-element.11.first_ref, bf16[2,160,512]{2,1,0:T(8,128)(2,1)} %bitcast.13, bf16[832,8192]{1,0:T(8,128)(2,1)} %all-gather.2.cloned.1.call-done.g_hbm, s32[2,160,1]{2,1,0:T(8,128)} %iota_add_fusion.qpos_ref, s32[2,160,1]{2,1,0:T(8,128)} %reshape.407.qseg_ref, ...), custom_call_target="tpu_custom_call" | custom-call | flops 6207569920 | bytes 19464192 | tf_op jit(solution)/shard_map/pallas_call | solution.py:148
  172.1 0.0 copy-start.1
  172.1 0.0 copy-start
  172.1 0.0 all-reduce.2.cloned.1.call-update
  172.1 0.6 copy-done.1
  172.8 0.1 copy.17
  172.9 0.1 reduce.1
  173.0 0.0 copy-done
  173.0 0.6 reshape.397.gain_ref
  173.7 0.1 fusion.3
  173.8 0.1 fusion.17
  173.9 0.0 slice-start
  173.9 2.5 slice-done
  176.4 4.1 %copy.18 = bf16[40,8,32,256]{3,2,1,0:T(8,128)(2,1)} copy(bf16[40,8,32,256]{3,1,2,0:T(8,128)(2,1)S(1)} %bitcast.9) | data formatting | bytes 10485760
  180.5 11.8 %gather_fusion = bf16[704,256]{1,0:T(8,128)(2,1)S(1)} fusion(bf16[320,32,256]{2,1,0:T(8,128)(2,1)} %bitcast.10, s32[704]{0:T(1024)S(1)} %fusion.17), kind=kCustom, calls=%fused_computation | custom fusion | bytes 726528 | tf_op jit(solution)/shard_map/gather | solution.py:233
  192.3 0.9 slice_select_fusion
  193.2 59.6 %all-reduce.2.cloned.1.call-done.projected_ref = bf16[320,8192]{1,0:T(8,128)(2,1)} async-done(((bf16[320,8192]{1,0:T(8,128)(2,1)}), bf16[320,8192]{1,0:T(8,128)(2,1)}) %all-reduce.2.cloned.1.call-update) | async-done | bytes 5242896 | tf_op jit(solution)/shard_map/psum | solution.py:223
  252.9 8.4 %shard_map.95 = bf16[320,8192]{1,0:T(8,128)(2,1)} custom-call(bf16[320,8192]{1,0:T(8,128)(2,1)} %all-reduce.2.cloned.1.call-done.projected_ref, bf16[320,8192]{1,0:T(8,128)(2,1)} %residual_ref.1, bf16[1,8192]{1,0:T(2,128)(2,1)} %reshape.397.gain_ref), custom_call_target="tpu_custom_call" | custom-call | flops 13107200 | bytes 15728640 | tf_op jit(solution)/shard_map/pallas_call | solution.py:173
  (9 shorter events, 0.2 us)
Async XLA Ops:
  7.2 138.4 %all-gather.2.cloned.1.call-start = ((), (), s32[]{:S(2)}) async-start(), calls=%async_computation | async-start | bytes 14057472 | tf_op jit(solution)/shard_map/all_gather | solution.py:196
  9.0 243.8 %all-reduce.2.cloned.1.call-start = ((), (), s32[]{:S(2)}) async-start(), calls=%async_computation.1 | async-start | bytes 10485760 | tf_op jit(solution)/shard_map/psum | solution.py:223
  172.1 0.7 copy-start.1
  172.1 0.9 copy-start
  173.9 2.5 slice-start
Sparse Core Ops, SparseCore 0:
  11.0 134.4 all-gather.1
  172.3 80.5 all-reduce.1

commit v8 on v7

--- a/solution.py
+++ b/solution.py
@@ -57,37 +57,51 @@
 
 
 def attn_kernel(
-    first_ref, q_ref, g_hbm, qpos_ref, qseg_ref, kpos_ref, kseg_ref, o_ref, window, sems,
+    first_ref, q_ref, g_hbm, qpos_ref, qseg_ref, kpos_ref, kseg_ref, o_ref, windows, sems,
     weight, weight_sem, attended, *, heads, scale, blocks, half, seq_count, kv_cols, weight_row,
+    count,
 ):
     step = pl.program_id(0)
-    first = first_ref[step]
     weight_copy = pltpu.make_async_copy(
         g_hbm.at[pl.ds(weight_row, weight.shape[0])], weight, weight_sem.at[0]
     )
 
+    def window_copies(slot):
+        first = first_ref[slot]
+        copies = []
+        for k in range(blocks):
+            block = first + k
+            upper = block >= seq_count
+            row = jnp.where(upper, half, 0)
+            device = jnp.where(upper, 2 * seq_count - 1 - block, block)
+            copies.append(
+                pltpu.make_async_copy(
+                    g_hbm.at[pl.ds(row, half), pl.ds(device * kv_cols, kv_cols)],
+                    windows.at[slot, pl.ds(k * half, half)],
+                    sems.at[slot, k],
+                )
+            )
+        return copies
+
+    pad = windows.shape[1] - blocks * half
+
     @pl.when(step == 0)
     def _():
+        for slot in range(count):
+            for copy in window_copies(slot):
+                copy.start()
+            if pad:
+                windows[slot, pl.ds(blocks * half, pad), :] = jnp.zeros((pad, kv_cols), windows.dtype)
         weight_copy.start()
 
-    copies = []
-    for k in range(blocks):
-        block = first + k
-        upper = block >= seq_count
-        row = jnp.where(upper, half, 0)
-        device = jnp.where(upper, 2 * seq_count - 1 - block, block)
-        copy = pltpu.make_async_copy(
-            g_hbm.at[pl.ds(row, half), pl.ds(device * kv_cols, kv_cols)],
-            window.at[pl.ds(k * half, half)],
-            sems.at[k],
-        )
-        copy.start()
-        copies.append(copy)
-    pad = window.shape[0] - blocks * half
-    if pad:
-        window[pl.ds(blocks * half, pad), :] = jnp.zeros((pad, kv_cols), window.dtype)
-    for copy in copies:
-        copy.wait()
+    for slot in range(count):
+
+        @pl.when(step == slot)
+        def _():
+            for copy in window_copies(slot):
+                copy.wait()
+
+    window = windows.at[step]
     allowed = (kpos_ref[0] <= qpos_ref[0]) & (kseg_ref[0] == qseg_ref[0])
     key = window[:, :HD]
     value = window[:, HD:]
@@ -123,7 +137,7 @@
     out_cols = gathered.shape[1]
     kern = functools.partial(
         attn_kernel, heads=heads, scale=1.0 / math.sqrt(HD), blocks=blocks, half=rows,
-        seq_count=seq_count, kv_cols=kv_cols, weight_row=weight_row,
+        seq_count=seq_count, kv_cols=kv_cols, weight_row=weight_row, count=count,
     )
     grid_spec = pltpu.PrefetchScalarGridSpec(
         num_scalar_prefetch=1,
@@ -138,8 +152,8 @@
         ],
         out_specs=pl.BlockSpec((1, rows, out_cols), lambda b, f: (b, 0, 0)),
         scratch_shapes=[
-            pltpu.VMEM((window_rows, kv_cols), gathered.dtype),
-            pltpu.SemaphoreType.DMA((blocks,)),
+            pltpu.VMEM((count, window_rows, kv_cols), gathered.dtype),
+            pltpu.SemaphoreType.DMA((count, blocks)),
             pltpu.VMEM((gathered.shape[0] - weight_row, out_cols), gathered.dtype),
             pltpu.SemaphoreType.DMA((1,)),
             pltpu.VMEM((rows, width), jnp.bfloat16),

time: 269 us -> 266 us (0.989)
  no operation moved by 1% of the time
where the time goes in v8:
time: 266 us
  waiting for transfers between devices  191 us (72%)
  Pallas kernels  32.6 us (12%)
  local copies, waits for them, and re-layouts  22.2 us (8%)
  between operations  14.1 us (5%)
  other arithmetic  5.91 us (2%)
    all_gather x1, waiting for transfers between devices, body(): lax.all_gather(jnp.concatenate([kv_rows, out_weight], axis=0), 'seq', axi...  131 us
    psum x1, waiting for transfers between devices, body(): projected = lax.psum(partial_value, 'tensor')  59.6 us
    pallas_call x1, Pallas kernels, attend(): pl.pallas_call(kern, grid_spec=grid_spec, out_shape=jax.ShapeDtypeStruct(...  24.2 us
    gather x1, local copies, waits for them, and re-layouts, body(): cache_rows = kv_grid[safe_index % per_device, safe_index // per_device]  11.8 us
    pallas_call x1, Pallas kernels, residual_norm(): pl.pallas_call(norm_kernel, grid=(steps,), in_specs=[pl.BlockSpec((rows_p...  8.42 us
  transfers between devices with their start and end apart: 2, of which 2 were waited for; matrix products, arithmetic and copies ran while one was open for 9% of the time, Pallas kernels for 0%

profile of v8, /device:TPU:1, one launch (start us, length us, event | category | flops | bytes accessed | tf_op | source)
XLA Modules:
  0.0 265.8 jit_solution(6849177918161693096)
XLA Ops:
  7.2 0.0 all-gather.2.cloned.1.call-start
  7.2 1.8 pad_maximum_fusion
  9.0 0.0 all-gather.2.cloned.1.call-update
  9.0 0.0 all-reduce.2.cloned.1.call-start
  9.1 0.7 broadcast_multiply_fusion
  9.8 0.1 add_select_fusion
  9.9 0.7 copy.15
  10.7 0.1 reduce
  10.8 0.3 convert_reduce_fusion
  11.1 0.7 reshape.395.kseg_ref
  11.7 0.1 iota_add_fusion.2
  11.8 0.1 add.242
  11.9 0.1 convert_reduce_fusion.1
  12.0 0.9 reshape.407.qseg_ref
  12.9 0.7 iota_add_fusion.qpos_ref
  13.6 0.7 broadcast_select_fusion.kpos_ref
  14.3 131.2 %all-gather.2.cloned.1.call-done.g_hbm = bf16[832,8192]{1,0:T(8,128)(2,1)} async-done(((bf16[832,256]{1,0:T(8,128)(2,1)}), bf16[832,8192]{1,0:T(8,128)(2,1)}) %all-gather.2.cloned.1.call-update) | async-done | bytes 13631504 | tf_op jit(solution)/shard_map/all_gather | solution.py:210
  145.5 24.2 %shard_map.94 = bf16[2,160,8192]{2,1,0:T(8,128)(2,1)} custom-call(s32[2]{0:T(128)} %get-tuple-element.11.first_ref, bf16[2,160,512]{2,1,0:T(8,128)(2,1)} %bitcast.13, bf16[832,8192]{1,0:T(8,128)(2,1)} %all-gather.2.cloned.1.call-done.g_hbm, s32[2,160,1]{2,1,0:T(8,128)} %iota_add_fusion.qpos_ref, s32[2,160,1]{2,1,0:T(8,128)} %reshape.407.qseg_ref, ...), custom_call_target="tpu_custom_call" | custom-call | flops 6207569920 | bytes 19464192 | tf_op jit(solution)/shard_map/pallas_call | solution.py:162
  169.7 0.0 copy-start.1
  169.7 0.0 copy-start
  169.8 0.0 all-reduce.2.cloned.1.call-update
  169.8 0.6 copy-done.1
  170.4 0.1 copy.17
  170.5 0.1 reduce.1
  170.7 0.0 copy-done
  170.7 0.6 reshape.397.gain_ref
  171.3 0.1 fusion.3
  171.4 0.1 fusion.17
  171.6 0.0 slice-start
  171.6 2.5 slice-done
  174.1 4.1 %copy.18 = bf16[40,8,32,256]{3,2,1,0:T(8,128)(2,1)} copy(bf16[40,8,32,256]{3,1,2,0:T(8,128)(2,1)S(1)} %bitcast.9) | data formatting | bytes 10485760
  178.1 11.8 %gather_fusion = bf16[704,256]{1,0:T(8,128)(2,1)S(1)} fusion(bf16[320,32,256]{2,1,0:T(8,128)(2,1)} %bitcast.10, s32[704]{0:T(1024)S(1)} %fusion.17), kind=kCustom, calls=%fused_computation | custom fusion | bytes 726528 | tf_op jit(solution)/shard_map/gather | solution.py:247
  190.0 0.9 slice_select_fusion
  190.9 59.6 %all-reduce.2.cloned.1.call-done.projected_ref = bf16[320,8192]{1,0:T(8,128)(2,1)} async-done(((bf16[320,8192]{1,0:T(8,128)(2,1)}), bf16[320,8192]{1,0:T(8,128)(2,1)}) %all-reduce.2.cloned.1.call-update) | async-done | bytes 5242896 | tf_op jit(solution)/shard_map/psum | solution.py:237
  250.5 8.4 %shard_map.95 = bf16[320,8192]{1,0:T(8,128)(2,1)} custom-call(bf16[320,8192]{1,0:T(8,128)(2,1)} %all-reduce.2.cloned.1.call-done.projected_ref, bf16[320,8192]{1,0:T(8,128)(2,1)} %residual_ref.1, bf16[1,8192]{1,0:T(2,128)(2,1)} %reshape.397.gain_ref), custom_call_target="tpu_custom_call" | custom-call | flops 13107200 | bytes 15728640 | tf_op jit(solution)/shard_map/pallas_call | solution.py:187
  (9 shorter events, 0.2 us)
Async XLA Ops:
  7.2 138.4 %all-gather.2.cloned.1.call-start = ((), (), s32[]{:S(2)}) async-start(), calls=%async_computation | async-start | bytes 14057472 | tf_op jit(solution)/shard_map/all_gather | solution.py:210
  9.0 241.5 %all-reduce.2.cloned.1.call-start = ((), (), s32[]{:S(2)}) async-start(), calls=%async_computation.1 | async-start | bytes 10485760 | tf_op jit(solution)/shard_map/psum | solution.py:237
  169.7 0.7 copy-start.1
  169.7 0.9 copy-start
  171.6 2.5 slice-start
Sparse Core Ops, SparseCore 0:
  11.0 134.4 all-gather.1
  169.9 80.5 all-reduce.1

commit v9 on v8

--- a/solution.py
+++ b/solution.py
@@ -112,7 +112,7 @@
         ) * scale
         scores = jnp.where(allowed, scores, -1e30)
         top = jnp.max(scores, axis=1, keepdims=True)
-        weights = jnp.where(allowed, jnp.exp(scores - top), 0.0)
+        weights = jnp.exp(scores - top)
         total = jnp.sum(weights, axis=1, keepdims=True)
         summed = jnp.dot(weights.astype(jnp.bfloat16), value, preferred_element_type=jnp.float32)
         attended[:, h * HD:(h + 1) * HD] = (summed / total).astype(attended.dtype)

time: 266 us -> 264 us (level)
  no operation moved by 1% of the time
where the time goes in v9:
time: 264 us
  waiting for transfers between devices  191 us (72%)
  Pallas kernels  30.7 us (12%)
  local copies, waits for them, and re-layouts  22.1 us (8%)
  between operations  14.1 us (5%)
  other arithmetic  5.91 us (2%)
    all_gather x1, waiting for transfers between devices, body(): lax.all_gather(jnp.concatenate([kv_rows, out_weight], axis=0), 'seq', axi...  131 us
    psum x1, waiting for transfers between devices, body(): projected = lax.psum(partial_value, 'tensor')  59.6 us
    pallas_call x1, Pallas kernels, attend(): pl.pallas_call(kern, grid_spec=grid_spec, out_shape=jax.ShapeDtypeStruct(...  22.3 us
    gather x1, local copies, waits for them, and re-layouts, body(): cache_rows = kv_grid[safe_index % per_device, safe_index // per_device]  11.8 us
    pallas_call x1, Pallas kernels, residual_norm(): pl.pallas_call(norm_kernel, grid=(steps,), in_specs=[pl.BlockSpec((rows_p...  8.42 us
  transfers between devices with their start and end apart: 2, of which 2 were waited for; matrix products, arithmetic and copies ran while one was open for 9% of the time, Pallas kernels for 0%

profile of v9, /device:TPU:1, one launch (start us, length us, event | category | flops | bytes accessed | tf_op | source)
XLA Modules:
  0.0 263.9 jit_solution(14592756450125016581)
XLA Ops:
  7.2 0.0 all-gather.2.cloned.1.call-start
  7.2 1.8 pad_maximum_fusion
  9.0 0.0 all-gather.2.cloned.1.call-update
  9.0 0.0 all-reduce.2.cloned.1.call-start
  9.1 0.7 broadcast_multiply_fusion
  9.8 0.1 add_select_fusion
  9.9 0.7 copy.15
  10.7 0.1 reduce
  10.8 0.3 convert_reduce_fusion
  11.1 0.7 reshape.395.kseg_ref
  11.7 0.1 iota_add_fusion.2
  11.8 0.1 add.242
  11.9 0.1 convert_reduce_fusion.1
  12.0 0.9 reshape.407.qseg_ref
  12.9 0.7 iota_add_fusion.qpos_ref
  13.6 0.7 broadcast_select_fusion.kpos_ref
  14.3 131.2 %all-gather.2.cloned.1.call-done.g_hbm = bf16[832,8192]{1,0:T(8,128)(2,1)} async-done(((bf16[832,256]{1,0:T(8,128)(2,1)}), bf16[832,8192]{1,0:T(8,128)(2,1)}) %all-gather.2.cloned.1.call-update) | async-done | bytes 13631504 | tf_op jit(solution)/shard_map/all_gather | solution.py:210
  145.5 22.3 %shard_map.94 = bf16[2,160,8192]{2,1,0:T(8,128)(2,1)} custom-call(s32[2]{0:T(128)} %get-tuple-element.11.first_ref, bf16[2,160,512]{2,1,0:T(8,128)(2,1)} %bitcast.13, bf16[832,8192]{1,0:T(8,128)(2,1)} %all-gather.2.cloned.1.call-done.g_hbm, s32[2,160,1]{2,1,0:T(8,128)} %iota_add_fusion.qpos_ref, s32[2,160,1]{2,1,0:T(8,128)} %reshape.407.qseg_ref, ...), custom_call_target="tpu_custom_call" | custom-call | flops 6207569920 | bytes 19464192 | tf_op jit(solution)/shard_map/pallas_call | solution.py:162
  167.9 0.0 copy-start.1
  167.9 0.0 copy-start
  167.9 0.0 all-reduce.2.cloned.1.call-update
  167.9 0.6 copy-done.1
  168.5 0.1 copy.17
  168.7 0.1 reduce.1
  168.8 0.0 copy-done
  168.8 0.6 reshape.397.gain_ref
  169.4 0.1 fusion.3
  169.6 0.1 fusion.17
  169.7 0.0 slice-start
  169.7 2.5 slice-done
  172.2 4.1 %copy.18 = bf16[40,8,32,256]{3,2,1,0:T(8,128)(2,1)} copy(bf16[40,8,32,256]{3,1,2,0:T(8,128)(2,1)S(1)} %bitcast.9) | data formatting | bytes 10485760
  176.3 11.8 %gather_fusion = bf16[704,256]{1,0:T(8,128)(2,1)S(1)} fusion(bf16[320,32,256]{2,1,0:T(8,128)(2,1)} %bitcast.10, s32[704]{0:T(1024)S(1)} %fusion.17), kind=kCustom, calls=%fused_computation | custom fusion | bytes 726528 | tf_op jit(solution)/shard_map/gather | solution.py:247
  188.1 0.9 slice_select_fusion
  189.0 59.6 %all-reduce.2.cloned.1.call-done.projected_ref = bf16[320,8192]{1,0:T(8,128)(2,1)} async-done(((bf16[320,8192]{1,0:T(8,128)(2,1)}), bf16[320,8192]{1,0:T(8,128)(2,1)}) %all-reduce.2.cloned.1.call-update) | async-done | bytes 5242896 | tf_op jit(solution)/shard_map/psum | solution.py:237
  248.6 8.4 %shard_map.95 = bf16[320,8192]{1,0:T(8,128)(2,1)} custom-call(bf16[320,8192]{1,0:T(8,128)(2,1)} %all-reduce.2.cloned.1.call-done.projected_ref, bf16[320,8192]{1,0:T(8,128)(2,1)} %residual_ref.1, bf16[1,8192]{1,0:T(2,128)(2,1)} %reshape.397.gain_ref), custom_call_target="tpu_custom_call" | custom-call | flops 13107200 | bytes 15728640 | tf_op jit(solution)/shard_map/pallas_call | solution.py:187
  (9 shorter events, 0.2 us)
Async XLA Ops:
  7.2 138.4 %all-gather.2.cloned.1.call-start = ((), (), s32[]{:S(2)}) async-start(), calls=%async_computation | async-start | bytes 14057472 | tf_op jit(solution)/shard_map/all_gather | solution.py:210
  9.0 239.6 %all-reduce.2.cloned.1.call-start = ((), (), s32[]{:S(2)}) async-start(), calls=%async_computation.1 | async-start | bytes 10485760 | tf_op jit(solution)/shard_map/psum | solution.py:237
  167.9 0.7 copy-start.1
  167.9 0.9 copy-start
  169.7 2.5 slice-start
Sparse Core Ops, SparseCore 0:
  11.0 134.4 all-gather.1
  168.0 80.5 all-reduce.1

commit v10 on v9

--- a/solution.py
+++ b/solution.py
@@ -181,7 +181,7 @@
     ).astype(out_ref.dtype)
 
 
-def residual_norm(projected, residual, gain, rows_per_step=80):
+def residual_norm(projected, residual, gain, rows_per_step=160):
     rows, width = projected.shape
     steps = rows // rows_per_step
     return pl.pallas_call(

time: 264 us -> 264 us (level)
  no operation moved by 1% of the time
where the time goes in v10:
time: 264 us; the launch traced here: 263 us
  waiting for transfers between devices  191 us (72%)
  Pallas kernels  30.2 us (11%)
  local copies, waits for them, and re-layouts  22.2 us (8%)
  between operations  14.1 us (5%)
  other arithmetic  5.91 us (2%)
    all_gather x1, waiting for transfers between devices, body(): lax.all_gather(jnp.concatenate([kv_rows, out_weight], axis=0), 'seq', axi...  131 us
    psum x1, waiting for transfers between devices, body(): projected = lax.psum(partial_value, 'tensor')  59.6 us
    pallas_call x1, Pallas kernels, attend(): pl.pallas_call(kern, grid_spec=grid_spec, out_shape=jax.ShapeDtypeStruct(...  22.3 us
    gather x1, local copies, waits for them, and re-layouts, body(): cache_rows = kv_grid[safe_index % per_device, safe_index // per_device]  11.8 us
    pallas_call x1, Pallas kernels, residual_norm(): pl.pallas_call(norm_kernel, grid=(steps,), in_specs=[pl.BlockSpec((rows_p...  7.9 us
  transfers between devices with their start and end apart: 2, of which 2 were waited for; matrix products, arithmetic and copies ran while one was open for 9% of the time, Pallas kernels for 0%

profile of v10, /device:TPU:1, one launch (start us, length us, event | category | flops | bytes accessed | tf_op | source)
XLA Modules:
  0.0 263.4 jit_solution(3159130693415156386)
XLA Ops:
  7.2 0.0 all-gather.2.cloned.1.call-start
  7.2 1.8 pad_maximum_fusion
  9.0 0.0 all-gather.2.cloned.1.call-update
  9.0 0.0 all-reduce.2.cloned.1.call-start
  9.1 0.7 broadcast_multiply_fusion
  9.8 0.1 add_select_fusion
  9.9 0.7 copy.15
  10.7 0.1 reduce
  10.8 0.3 convert_reduce_fusion
  11.1 0.7 reshape.395.kseg_ref
  11.7 0.1 iota_add_fusion.2
  11.8 0.1 add.242
  11.9 0.1 convert_reduce_fusion.1
  12.0 0.9 reshape.407.qseg_ref
  12.9 0.7 iota_add_fusion.qpos_ref
  13.6 0.7 broadcast_select_fusion.kpos_ref
  14.3 131.2 %all-gather.2.cloned.1.call-done.g_hbm = bf16[832,8192]{1,0:T(8,128)(2,1)} async-done(((bf16[832,256]{1,0:T(8,128)(2,1)}), bf16[832,8192]{1,0:T(8,128)(2,1)}) %all-gather.2.cloned.1.call-update) | async-done | bytes 13631504 | tf_op jit(solution)/shard_map/all_gather | solution.py:210
  145.5 22.3 %shard_map.94 = bf16[2,160,8192]{2,1,0:T(8,128)(2,1)} custom-call(s32[2]{0:T(128)} %get-tuple-element.11.first_ref, bf16[2,160,512]{2,1,0:T(8,128)(2,1)} %bitcast.13, bf16[832,8192]{1,0:T(8,128)(2,1)} %all-gather.2.cloned.1.call-done.g_hbm, s32[2,160,1]{2,1,0:T(8,128)} %iota_add_fusion.qpos_ref, s32[2,160,1]{2,1,0:T(8,128)} %reshape.407.qseg_ref, ...), custom_call_target="tpu_custom_call" | custom-call | flops 6207569920 | bytes 19464192 | tf_op jit(solution)/shard_map/pallas_call | solution.py:162
  167.9 0.0 copy-start.1
  167.9 0.0 copy-start
  167.9 0.0 all-reduce.2.cloned.1.call-update
  167.9 0.6 copy-done.1
  168.5 0.1 copy.17
  168.7 0.1 reduce.1
  168.8 0.0 copy-done
  168.8 0.6 reshape.397.gain_ref
  169.4 0.1 fusion.3
  169.6 0.1 fusion.17
  169.7 0.0 slice-start
  169.7 2.5 slice-done
  172.2 4.1 %copy.18 = bf16[40,8,32,256]{3,2,1,0:T(8,128)(2,1)} copy(bf16[40,8,32,256]{3,1,2,0:T(8,128)(2,1)S(1)} %bitcast.9) | data formatting | bytes 10485760
  176.3 11.8 %gather_fusion = bf16[704,256]{1,0:T(8,128)(2,1)S(1)} fusion(bf16[320,32,256]{2,1,0:T(8,128)(2,1)} %bitcast.10, s32[704]{0:T(1024)S(1)} %fusion.17), kind=kCustom, calls=%fused_computation | custom fusion | bytes 726528 | tf_op jit(solution)/shard_map/gather | solution.py:247
  188.1 0.9 slice_select_fusion
  189.0 59.6 %all-reduce.2.cloned.1.call-done.projected_ref = bf16[320,8192]{1,0:T(8,128)(2,1)} async-done(((bf16[320,8192]{1,0:T(8,128)(2,1)}), bf16[320,8192]{1,0:T(8,128)(2,1)}) %all-reduce.2.cloned.1.call-update) | async-done | bytes 5242896 | tf_op jit(solution)/shard_map/psum | solution.py:237
  248.6 7.9 %shard_map.95 = bf16[320,8192]{1,0:T(8,128)(2,1)} custom-call(bf16[320,8192]{1,0:T(8,128)(2,1)} %all-reduce.2.cloned.1.call-done.projected_ref, bf16[320,8192]{1,0:T(8,128)(2,1)} %residual_ref.1, bf16[1,8192]{1,0:T(2,128)(2,1)} %reshape.397.gain_ref), custom_call_target="tpu_custom_call" | custom-call | flops 13107200 | bytes 15728640 | tf_op jit(solution)/shard_map/pallas_call | solution.py:187
  (9 shorter events, 0.2 us)
Async XLA Ops:
  7.2 138.4 %all-gather.2.cloned.1.call-start = ((), (), s32[]{:S(2)}) async-start(), calls=%async_computation | async-start | bytes 14057472 | tf_op jit(solution)/shard_map/all_gather | solution.py:210
  9.0 239.6 %all-reduce.2.cloned.1.call-start = ((), (), s32[]{:S(2)}) async-start(), calls=%async_computation.1 | async-start | bytes 10485760 | tf_op jit(solution)/shard_map/psum | solution.py:237
  167.9 0.7 copy-start.1
  167.9 0.9 copy-start
  169.7 2.5 slice-start
Sparse Core Ops, SparseCore 0:
  11.0 134.4 all-gather.1
  168.0 80.5 all-reduce.1

commit v11 on v9

--- a/solution.py
+++ b/solution.py
@@ -122,7 +122,7 @@
         weight_copy.wait()
 
     out_cols = o_ref.shape[2]
-    chunk = 1024 if out_cols % 1024 == 0 else out_cols
+    chunk = 2048 if out_cols % 2048 == 0 else out_cols
     for c in range(out_cols // chunk):
         o_ref[0, :, c * chunk:(c + 1) * chunk] = jnp.dot(
             attended[...], weight[:, c * chunk:(c + 1) * chunk], preferred_element_type=jnp.float32

time: 264 us -> 264 us (level)
  no operation moved by 1% of the time
where the time goes in v11:
time: 264 us
  waiting for transfers between devices  191 us (72%)
  Pallas kernels  30.7 us (12%)
  local copies, waits for them, and re-layouts  22.1 us (8%)
  between operations  14.1 us (5%)
  other arithmetic  5.91 us (2%)
    all_gather x1, waiting for transfers between devices, body(): lax.all_gather(jnp.concatenate([kv_rows, out_weight], axis=0), 'seq', axi...  131 us
    psum x1, waiting for transfers between devices, body(): projected = lax.psum(partial_value, 'tensor')  59.6 us
    pallas_call x1, Pallas kernels, attend(): pl.pallas_call(kern, grid_spec=grid_spec, out_shape=jax.ShapeDtypeStruct(...  22.3 us
    gather x1, local copies, waits for them, and re-layouts, body(): cache_rows = kv_grid[safe_index % per_device, safe_index // per_device]  11.8 us
    pallas_call x1, Pallas kernels, residual_norm(): pl.pallas_call(norm_kernel, grid=(steps,), in_specs=[pl.BlockSpec((rows_p...  8.42 us
  transfers between devices with their start and end apart: 2, of which 2 were waited for; matrix products, arithmetic and copies ran while one was open for 9% of the time, Pallas kernels for 0%

profile of v11, /device:TPU:1, one launch (start us, length us, event | category | flops | bytes accessed | tf_op | source)
XLA Modules:
  0.0 263.9 jit_solution(10378508011264042396)
XLA Ops:
  7.2 0.0 all-gather.2.cloned.1.call-start
  7.2 1.8 pad_maximum_fusion
  9.0 0.0 all-gather.2.cloned.1.call-update
  9.0 0.0 all-reduce.2.cloned.1.call-start
  9.1 0.7 broadcast_multiply_fusion
  9.8 0.1 add_select_fusion
  9.9 0.7 copy.15
  10.7 0.1 reduce
  10.8 0.3 convert_reduce_fusion
  11.1 0.7 reshape.395.kseg_ref
  11.7 0.1 iota_add_fusion.2
  11.8 0.1 add.242
  11.9 0.1 convert_reduce_fusion.1
  12.0 0.9 reshape.407.qseg_ref
  12.9 0.7 iota_add_fusion.qpos_ref
  13.6 0.7 broadcast_select_fusion.kpos_ref
  14.3 131.2 %all-gather.2.cloned.1.call-done.g_hbm = bf16[832,8192]{1,0:T(8,128)(2,1)} async-done(((bf16[832,256]{1,0:T(8,128)(2,1)}), bf16[832,8192]{1,0:T(8,128)(2,1)}) %all-gather.2.cloned.1.call-update) | async-done | bytes 13631504 | tf_op jit(solution)/shard_map/all_gather | solution.py:210
  145.5 22.3 %shard_map.94 = bf16[2,160,8192]{2,1,0:T(8,128)(2,1)} custom-call(s32[2]{0:T(128)} %get-tuple-element.11.first_ref, bf16[2,160,512]{2,1,0:T(8,128)(2,1)} %bitcast.13, bf16[832,8192]{1,0:T(8,128)(2,1)} %all-gather.2.cloned.1.call-done.g_hbm, s32[2,160,1]{2,1,0:T(8,128)} %iota_add_fusion.qpos_ref, s32[2,160,1]{2,1,0:T(8,128)} %reshape.407.qseg_ref, ...), custom_call_target="tpu_custom_call" | custom-call | flops 6207569920 | bytes 19464192 | tf_op jit(solution)/shard_map/pallas_call | solution.py:162
  167.9 0.0 copy-start.1
  167.9 0.0 copy-start
  167.9 0.0 all-reduce.2.cloned.1.call-update
  167.9 0.6 copy-done.1
  168.5 0.1 copy.17
  168.7 0.1 reduce.1
  168.8 0.0 copy-done
  168.8 0.6 reshape.397.gain_ref
  169.4 0.1 fusion.3
  169.6 0.1 fusion.17
  169.7 0.0 slice-start
  169.7 2.5 slice-done
  172.2 4.1 %copy.18 = bf16[40,8,32,256]{3,2,1,0:T(8,128)(2,1)} copy(bf16[40,8,32,256]{3,1,2,0:T(8,128)(2,1)S(1)} %bitcast.9) | data formatting | bytes 10485760
  176.3 11.8 %gather_fusion = bf16[704,256]{1,0:T(8,128)(2,1)S(1)} fusion(bf16[320,32,256]{2,1,0:T(8,128)(2,1)} %bitcast.10, s32[704]{0:T(1024)S(1)} %fusion.17), kind=kCustom, calls=%fused_computation | custom fusion | bytes 726528 | tf_op jit(solution)/shard_map/gather | solution.py:247
  188.1 0.9 slice_select_fusion
  189.0 59.6 %all-reduce.2.cloned.1.call-done.projected_ref = bf16[320,8192]{1,0:T(8,128)(2,1)} async-done(((bf16[320,8192]{1,0:T(8,128)(2,1)}), bf16[320,8192]{1,0:T(8,128)(2,1)}) %all-reduce.2.cloned.1.call-update) | async-done | bytes 5242896 | tf_op jit(solution)/shard_map/psum | solution.py:237
  248.7 8.4 %shard_map.95 = bf16[320,8192]{1,0:T(8,128)(2,1)} custom-call(bf16[320,8192]{1,0:T(8,128)(2,1)} %all-reduce.2.cloned.1.call-done.projected_ref, bf16[320,8192]{1,0:T(8,128)(2,1)} %residual_ref.1, bf16[1,8192]{1,0:T(2,128)(2,1)} %reshape.397.gain_ref), custom_call_target="tpu_custom_call" | custom-call | flops 13107200 | bytes 15728640 | tf_op jit(solution)/shard_map/pallas_call | solution.py:187
  (9 shorter events, 0.2 us)
Async XLA Ops:
  7.2 138.4 %all-gather.2.cloned.1.call-start = ((), (), s32[]{:S(2)}) async-start(), calls=%async_computation | async-start | bytes 14057472 | tf_op jit(solution)/shard_map/all_gather | solution.py:210
  9.0 239.6 %all-reduce.2.cloned.1.call-start = ((), (), s32[]{:S(2)}) async-start(), calls=%async_computation.1 | async-start | bytes 10485760 | tf_op jit(solution)/shard_map/psum | solution.py:237
  167.9 0.7 copy-start.1
  167.9 0.9 copy-start
  169.7 2.5 slice-start
Sparse Core Ops, SparseCore 0:
  11.0 134.4 all-gather.1
  168.0 80.5 all-reduce.1

commit v12 on v9

--- a/solution.py
+++ b/solution.py
@@ -102,11 +102,17 @@
                 copy.wait()
 
     window = windows.at[step]
-    allowed = (kpos_ref[0] <= qpos_ref[0]) & (kseg_ref[0] == qseg_ref[0])
+    pair = 2 if heads % 2 == 0 else 1
+    rows = q_ref.shape[1]
+    query_position = jnp.concatenate([qpos_ref[0]] * pair, axis=0)
+    query_segment = jnp.concatenate([qseg_ref[0]] * pair, axis=0)
+    allowed = (kpos_ref[0] <= query_position) & (kseg_ref[0] == query_segment)
     key = window[:, :HD]
     value = window[:, HD:]
-    for h in range(heads):
-        query = q_ref[0, :, h * HD:(h + 1) * HD]
+    for g in range(heads // pair):
+        query = jnp.concatenate(
+            [q_ref[0, :, (g * pair + p) * HD:(g * pair + p + 1) * HD] for p in range(pair)], axis=0
+        )
         scores = lax.dot_general(
             query, key, (((1,), (1,)), ((), ())), preferred_element_type=jnp.float32
         ) * scale
@@ -115,7 +121,10 @@
         weights = jnp.exp(scores - top)
         total = jnp.sum(weights, axis=1, keepdims=True)
         summed = jnp.dot(weights.astype(jnp.bfloat16), value, preferred_element_type=jnp.float32)
-        attended[:, h * HD:(h + 1) * HD] = (summed / total).astype(attended.dtype)
+        result = (summed / total).astype(attended.dtype)
+        for p in range(pair):
+            h = g * pair + p
+            attended[:, h * HD:(h + 1) * HD] = result[p * rows:(p + 1) * rows]
 
     @pl.when(step == 0)
     def _():

time: 264 us -> 267 us (1.011)
  Pallas kernels: 30.7 us -> 33.4 us
    pallas_call x1, Pallas kernels: 22.3 us -> 25 us  [attend(): pl.pallas_call(kern, grid_spec=grid_spec, out_shape=jax.ShapeDtypeStruct(...]
where the time goes in v12:
time: 267 us
  waiting for transfers between devices  191 us (72%)
  Pallas kernels  33.4 us (13%)
  local copies, waits for them, and re-layouts  22.2 us (8%)
  between operations  14.1 us (5%)
  other arithmetic  5.91 us (2%)
    all_gather x1, waiting for transfers between devices, body(): lax.all_gather(jnp.concatenate([kv_rows, out_weight], axis=0), 'seq', axi...  131 us
    psum x1, waiting for transfers between devices, body(): projected = lax.psum(partial_value, 'tensor')  59.6 us
    pallas_call x1, Pallas kernels, attend(): pl.pallas_call(kern, grid_spec=grid_spec, out_shape=jax.ShapeDtypeStruct(...  25 us
    gather x1, local copies, waits for them, and re-layouts, body(): cache_rows = kv_grid[safe_index % per_device, safe_index // per_device]  11.8 us
    pallas_call x1, Pallas kernels, residual_norm(): pl.pallas_call(norm_kernel, grid=(steps,), in_specs=[pl.BlockSpec((rows_p...  8.42 us
  transfers between devices with their start and end apart: 2, of which 2 were waited for; matrix products, arithmetic and copies ran while one was open for 9% of the time, Pallas kernels for 0%

profile of v12, /device:TPU:1, one launch (start us, length us, event | category | flops | bytes accessed | tf_op | source)
XLA Modules:
  0.0 266.6 jit_solution(14009895120343343934)
XLA Ops:
  7.2 0.0 all-gather.2.cloned.1.call-start
  7.2 1.8 pad_maximum_fusion
  9.0 0.0 all-gather.2.cloned.1.call-update
  9.0 0.0 all-reduce.2.cloned.1.call-start
  9.1 0.7 broadcast_multiply_fusion
  9.8 0.1 add_select_fusion
  9.9 0.7 copy.15
  10.7 0.1 reduce
  10.8 0.3 convert_reduce_fusion
  11.1 0.7 reshape.395.kseg_ref
  11.7 0.1 iota_add_fusion.2
  11.8 0.1 add.242
  11.9 0.1 convert_reduce_fusion.1
  12.0 0.9 reshape.407.qseg_ref
  12.9 0.7 iota_add_fusion.qpos_ref
  13.6 0.7 broadcast_select_fusion.kpos_ref
  14.3 131.2 %all-gather.2.cloned.1.call-done.g_hbm = bf16[832,8192]{1,0:T(8,128)(2,1)} async-done(((bf16[832,256]{1,0:T(8,128)(2,1)}), bf16[832,8192]{1,0:T(8,128)(2,1)}) %all-gather.2.cloned.1.call-update) | async-done | bytes 13631504 | tf_op jit(solution)/shard_map/all_gather | solution.py:219
  145.5 25.0 %shard_map.94 = bf16[2,160,8192]{2,1,0:T(8,128)(2,1)} custom-call(s32[2]{0:T(128)} %get-tuple-element.11.first_ref, bf16[2,160,512]{2,1,0:T(8,128)(2,1)} %bitcast.13, bf16[832,8192]{1,0:T(8,128)(2,1)} %all-gather.2.cloned.1.call-done.g_hbm, s32[2,160,1]{2,1,0:T(8,128)} %iota_add_fusion.qpos_ref, s32[2,160,1]{2,1,0:T(8,128)} %reshape.407.qseg_ref, ...), custom_call_target="tpu_custom_call" | custom-call | flops 6207569920 | bytes 19464192 | tf_op jit(solution)/shard_map/pallas_call | solution.py:171
  170.5 0.0 copy-start.1
  170.5 0.0 copy-start
  170.6 0.0 all-reduce.2.cloned.1.call-update
  170.6 0.6 copy-done.1
  171.2 0.1 copy.17
  171.3 0.1 reduce.1
  171.5 0.0 copy-done
  171.5 0.6 reshape.397.gain_ref
  172.1 0.1 fusion.3
  172.2 0.1 fusion.17
  172.4 0.0 slice-start
  172.4 2.5 slice-done
  174.9 4.1 %copy.18 = bf16[40,8,32,256]{3,2,1,0:T(8,128)(2,1)} copy(bf16[40,8,32,256]{3,1,2,0:T(8,128)(2,1)S(1)} %bitcast.9) | data formatting | bytes 10485760
  178.9 11.8 %gather_fusion = bf16[704,256]{1,0:T(8,128)(2,1)S(1)} fusion(bf16[320,32,256]{2,1,0:T(8,128)(2,1)} %bitcast.10, s32[704]{0:T(1024)S(1)} %fusion.17), kind=kCustom, calls=%fused_computation | custom fusion | bytes 726528 | tf_op jit(solution)/shard_map/gather | solution.py:256
  190.8 0.9 slice_select_fusion
  191.7 59.6 %all-reduce.2.cloned.1.call-done.projected_ref = bf16[320,8192]{1,0:T(8,128)(2,1)} async-done(((bf16[320,8192]{1,0:T(8,128)(2,1)}), bf16[320,8192]{1,0:T(8,128)(2,1)}) %all-reduce.2.cloned.1.call-update) | async-done | bytes 5242896 | tf_op jit(solution)/shard_map/psum | solution.py:246
  251.3 8.4 %shard_map.95 = bf16[320,8192]{1,0:T(8,128)(2,1)} custom-call(bf16[320,8192]{1,0:T(8,128)(2,1)} %all-reduce.2.cloned.1.call-done.projected_ref, bf16[320,8192]{1,0:T(8,128)(2,1)} %residual_ref.1, bf16[1,8192]{1,0:T(2,128)(2,1)} %reshape.397.gain_ref), custom_call_target="tpu_custom_call" | custom-call | flops 13107200 | bytes 15728640 | tf_op jit(solution)/shard_map/pallas_call | solution.py:196
  (9 shorter events, 0.2 us)
Async XLA Ops:
  7.2 138.4 %all-gather.2.cloned.1.call-start = ((), (), s32[]{:S(2)}) async-start(), calls=%async_computation | async-start | bytes 14057472 | tf_op jit(solution)/shard_map/all_gather | solution.py:219
  9.0 242.3 %all-reduce.2.cloned.1.call-start = ((), (), s32[]{:S(2)}) async-start(), calls=%async_computation.1 | async-start | bytes 10485760 | tf_op jit(solution)/shard_map/psum | solution.py:246
  170.5 0.7 copy-start.1
  170.5 0.9 copy-start
  172.4 2.5 slice-start
Sparse Core Ops, SparseCore 0:
  11.0 134.4 all-gather.1
  170.7 80.5 all-reduce.1
